TPU v7x, 512 devices: a whole 4x4x16 slice. The times are simulated.
512 devices in a mesh: dir: 8 (over z_lo), row: 64 (over x, y, z_hi, core).
Axes of the slice: x: 4, y: 4, z: 16 (z_hi: 2, z_lo: 8; z = z_hi * 8 + z_lo), core: 2. Of those that a mesh axis runs over, the one named last changes fastest.
Arguments:
- white_noise: bfloat16 [2, 8192, 8192], P(None, ('dir', 'row')), may hold values from -6 to 6
- geometry: int32 [8, 2], P('dir'), may hold values from 0 to 3
- window: int32 [8], P('dir'), may hold values from 1 to 8, as said below
- tile_map: int32 [8, 8192], P('dir'), may hold values from 0 to 65535
- link_gain: float32 [8, 8192], P('dir'), may hold values from 0.1 to 1
- serving: int32 [8192], replicated, may hold values from 0 to 7
Outputs:
- fluctuation: float32 [8, 512, 128], P('dir', 'row')
- signal_ratio: float32 [8192], P(('dir', 'row'))
Inputs may be any that keep to these rules, and one draw needn't show every extreme that they name: geometry[d,0] is direction d's Fresnel-scale bin and geometry[d,1] its slant bin. `window`: some direction has the half-width 8. `tile_map`: tile (t,u) is numbered t * 128 + u.
All inputs are finite; a program needn't handle non-finite values.
Results may differ from a plain program's by a relative error of at most 0.034.
Values may be sent and summed in bfloat16 or wider, within the bound.
No kernel may reach another device: no remote copies, remote signals or barrier semaphores. Data moves between devices by JAX's collectives and lax.ppermute only.
A program may use at most 64 MiB of HBM per device.

v0:
```python
import math

import jax
import jax.numpy as jnp
from jax import lax
from jax.sharding import PartitionSpec as P

N = 8192
FIRST = 64
SECOND = 128
ROWS_DEV = 32
XTILES = 128
YTILES = 8
TILE_X = 64


full_turn = 2.0 * math.pi
noise_floor = 0.05
tiny_value = 1e-06
strength = 1.6
row_patterns = (
    "zrab,zwak->wrkb",
    "zrkb,zwbc->wrkc",
    "zrkc,wzbc->wrkb",
    "zrkb,wzak->wrab",
    "zrkb,zak->rab",
)
column_patterns = (
    "zaby,zwak->wkby",
    "zkby,zwbc->wkcy",
    "zkcy,wzbc->wkby",
    "zkby,wzak->waby",
    "zkby,zak->aby",
)


def complex_block(real_part, imag_part):
    return jnp.stack(
        [jnp.stack([real_part, imag_part]), jnp.stack([-imag_part, real_part])]
    ).astype(jnp.bfloat16)


def transform_tables(first, second):
    total = first * second
    outer_ids = jnp.arange(first, dtype=jnp.int32)
    inner_ids = jnp.arange(second, dtype=jnp.int32)
    outer_angle = (outer_ids[:, None] * outer_ids[None, :] % first).astype(jnp.float32) * (
        full_turn / first
    )
    inner_angle = (inner_ids[:, None] * inner_ids[None, :] % second).astype(jnp.float32) * (
        full_turn / second
    )
    twist_angle = (outer_ids[:, None] * inner_ids[None, :] % total).astype(jnp.float32) * (
        full_turn / total
    )
    return (
        complex_block(jnp.cos(outer_angle), -jnp.sin(outer_angle)),
        complex_block(jnp.cos(inner_angle), -jnp.sin(inner_angle)),
        jnp.cos(twist_angle),
        -jnp.sin(twist_angle),
    )


def signed_wave(positions, first, second):
    total = first * second
    wave_number = positions // second + first * (positions % second)
    return jnp.where(wave_number >= total // 2, wave_number - total, wave_number).astype(
        jnp.float32
    )


def spectral_filter(row_ids, column_ids):
    wave_rows = signed_wave(row_ids, FIRST, SECOND)
    wave_columns = signed_wave(column_ids, FIRST, SECOND)
    squared_radius = 16.0 + wave_rows[:, None] ** 2 + wave_columns[None, :] ** 2
    return strength * float(N) * float(N) * squared_radius ** (-0.75)


def fresnel_factor(geometry_row, first, second):
    total = first * second
    fresnel_area = 144.0 * jnp.exp2(geometry_row[0].astype(jnp.float32))
    positions = jnp.arange(total, dtype=jnp.int32).reshape(first, second)
    scaled = signed_wave(positions, first, second) * (full_turn / total)
    turning = 0.5 * scaled * scaled * fresnel_area
    return (jnp.cos(turning), -jnp.sin(turning))


def complex_times(values, real_part, imag_part):
    return jnp.stack(
        [
            values[0] * real_part - values[1] * imag_part,
            values[0] * imag_part + values[1] * real_part,
        ]
    )


def contract(pattern, operand, matrix):
    return jnp.einsum(pattern, operand, matrix, preferred_element_type=jnp.float32)


def table_length(tables):
    return tables[0].shape[2] * tables[1].shape[2]


def forward_axis(values, tables, factor, patterns, trailing):
    outer_table, inner_table, twist_real, twist_imag = tables
    factor_real, factor_imag = factor
    if trailing:
        twist_real, twist_imag = (twist_real[..., None], twist_imag[..., None])
        factor_real, factor_imag = (factor_real[..., None], factor_imag[..., None])
    section_one = complex_times(
        contract(patterns[0], values, outer_table), twist_real, twist_imag
    ).astype(jnp.bfloat16)
    section_two = contract(patterns[1], section_one, inner_table)
    return complex_times(section_two, factor_real, factor_imag).astype(jnp.bfloat16)


def inverse_first(values, tables, patterns, trailing):
    outer_table, inner_table, twist_real, twist_imag = tables
    if trailing:
        twist_real, twist_imag = (twist_real[..., None], twist_imag[..., None])
    return complex_times(
        contract(patterns[2], values, inner_table), twist_real, -twist_imag
    ).astype(jnp.bfloat16)


def inverse_axis(values, tables, patterns, trailing):
    section_one = inverse_first(values, tables, patterns, trailing)
    return contract(patterns[3], section_one, tables[0]) * (1.0 / table_length(tables))


def window_matrix(half_width):
    positions = jnp.arange(XTILES, dtype=jnp.int32)
    difference = (positions[:, None] - positions[None, :]) % XTILES
    distance = jnp.minimum(difference, XTILES - difference)
    return (distance <= half_width).astype(jnp.float32)


def tile_statistics(first_moment, second_moment, half_width, tile_rows):
    window_mask = window_matrix(half_width)
    cells = ((2 * half_width + 1) * (TILE_X * tile_rows)).astype(jnp.float32)
    mean_one = jnp.dot(first_moment, window_mask, precision=lax.Precision.HIGHEST) / cells
    mean_two = jnp.dot(second_moment, window_mask, precision=lax.Precision.HIGHEST) / cells
    fluctuation = mean_two / (mean_one * mean_one + tiny_value) - 1.0
    return (fluctuation, mean_one * jnp.exp(-fluctuation))


def propagate_columns(phase_patch, tables_y, slant_factor, fresnel_y):
    patch_rows = phase_patch.shape[0]
    width_here = phase_patch.shape[1]
    outer_len = tables_y[0].shape[2]
    inner_len = tables_y[1].shape[2]
    turned_phase = slant_factor * phase_patch
    screen_field = jnp.stack([jnp.cos(turned_phase), jnp.sin(turned_phase)]).astype(jnp.bfloat16)
    stacked = screen_field.reshape(2, outer_len, inner_len, width_here)
    spectral = forward_axis(stacked, tables_y, fresnel_y, column_patterns, True)
    result = inverse_axis(spectral, tables_y, column_patterns, True)
    return result.astype(jnp.bfloat16).reshape(2, patch_rows, width_here)


def body(white_noise, geometry, window, tile_map, link_gain, serving):
    row_count = lax.axis_size("row")
    tables = transform_tables(FIRST, SECOND)
    tables_y = transform_tables(row_count, ROWS_DEV)
    patch_len = row_count * ROWS_DEV
    rows_here = white_noise.shape[1]
    row_start = lax.axis_index(("dir", "row")) * rows_here
    row_ids = row_start + jnp.arange(rows_here, dtype=jnp.int32)
    column_ids = jnp.arange(N, dtype=jnp.int32)
    spectral_gain = spectral_filter(row_ids, column_ids)
    spectrum = (white_noise.astype(jnp.float32) * spectral_gain).astype(jnp.bfloat16)
    half_screen = inverse_axis(
        spectrum.reshape(2, rows_here, FIRST, SECOND), tables, row_patterns, False
    )
    half_screen = half_screen.astype(jnp.bfloat16).reshape(2, rows_here, N)
    turned = lax.all_to_all(half_screen, "row", split_axis=2, concat_axis=1, tiled=True)
    band_rows = turned.shape[1]
    columns = turned.shape[2]
    slant_factor = 1.0 + 0.25 * geometry[0, 1].astype(jnp.float32)
    fresnel_x = fresnel_factor(geometry[0], FIRST, SECOND)
    fresnel_y = fresnel_factor(geometry[0], row_count, ROWS_DEV)
    offset_rows = N // 4 * geometry[0, 1]
    blocks = band_rows // SECOND
    block_start = lax.axis_index("dir") * blocks
    stacked = turned.reshape(2, blocks, SECOND, columns)
    twist_real = lax.dynamic_slice_in_dim(tables[2], block_start, blocks, 0)[..., None]
    twist_imag = lax.dynamic_slice_in_dim(tables[3], block_start, blocks, 0)[..., None]
    section_one = complex_times(
        contract("zkcx,wzbc->wkbx", stacked, tables[1]), twist_real, -twist_imag
    )
    section_one = section_one.astype(jnp.bfloat16)
    outer_count = patch_len // SECOND
    outer_ids = (offset_rows // SECOND + jnp.arange(outer_count, dtype=jnp.int32)) % FIRST
    patch_outer = jnp.take(tables[0][0], outer_ids, axis=1)
    phase_patch = contract(
        "zkbx,zak->abx", lax.all_gather(section_one, "dir", axis=1, tiled=True), patch_outer
    )
    phase_patch = phase_patch.reshape(patch_len, columns) * (1.0 / N)
    screen_field = propagate_columns(phase_patch, tables_y, slant_factor, fresnel_y)
    stacked_field = screen_field.reshape(2, row_count, ROWS_DEV, columns)
    portion = lax.all_to_all(stacked_field, "row", split_axis=1, concat_axis=3, tiled=True)
    item_count = portion.shape[2]
    stacked = portion.reshape(2, item_count, FIRST, SECOND)
    spectral = forward_axis(stacked, tables, fresnel_x, row_patterns, False)
    wave_field = inverse_axis(spectral, tables, row_patterns, False)
    intensity = wave_field[0] * wave_field[0] + wave_field[1] * wave_field[1]
    intensity = intensity.reshape(item_count, XTILES, TILE_X)
    tile_one = jnp.sum(intensity, axis=2)
    tile_two = jnp.sum(intensity * intensity, axis=2)
    tile_rows = ROWS_DEV // YTILES
    first_moment = jnp.sum(tile_one.reshape(YTILES, tile_rows, XTILES), axis=1)
    second_moment = jnp.sum(tile_two.reshape(YTILES, tile_rows, XTILES), axis=1)
    fluctuation, faded_power = tile_statistics(first_moment, second_moment, window[0], tile_rows)
    faded_flat = faded_power.reshape(-1)
    tile_total = faded_flat.shape[0]
    local_tile = tile_map[0] - lax.axis_index("row") * tile_total
    inside = (local_tile >= 0) & (local_tile < tile_total)
    looked = jnp.where(inside, jnp.take(faded_flat, jnp.clip(local_tile, 0, tile_total - 1)), 0.0)
    received = link_gain[0] * looked
    direction = lax.axis_index("dir")
    serves_here = serving == direction
    signal_part = jnp.where(serves_here, received, 0.0)
    interference_part = jnp.where(serves_here, 0.0, received)
    signal, interference = lax.psum((signal_part, interference_part), ("dir", "row"))
    share_size = serving.shape[0] // lax.axis_size(("dir", "row"))
    share_start = lax.axis_index(("dir", "row")) * share_size
    signal = lax.dynamic_slice_in_dim(signal, share_start, share_size, 0)
    interference = lax.dynamic_slice_in_dim(interference, share_start, share_size, 0)
    signal_ratio = jnp.log10(signal / (interference + noise_floor))
    return (fluctuation[None], signal_ratio)


def solution(mesh):
    return jax.shard_map(
        body,
        mesh=mesh,
        in_specs=(
            P(None, ("dir", "row"), None),
            P("dir", None),
            P("dir"),
            P("dir", None),
            P("dir", None),
            P(),
        ),
        out_specs=(P("dir", "row", None), P(("dir", "row"))),
        check_vma=False,
    )
```

profile of v0, /device:TPU:1, one launch (start us, length us, event | category | flops | bytes accessed | tf_op | source)
XLA Modules:
  0.0 767.3 jit_solution(9661457028871132074)
XLA Ops:
  8.5 1.1 multiply_convert_fusion
  10.7 4.7 copy.193
  15.4 12.9 %reshape.910 = bf16[64,2,2048]{2,1,0:T(2,128)(2,1)} reshape(bf16[8192,2,16]{2,1,0:T(2,128)(2,1)} %bitcast.208) | data formatting | bytes 1048576
  28.3 22.2 %all-to-all-start = ((bf16[64,2,2048]{2,1,0:T(2,128)(2,1)}), bf16[64,2,2048]{2,1,0:T(2,128)(2,1)S(1)}, u32[]{:S(2)}, u32[]{:S(2)}) async-start(bf16[64,2,2048]{2,1,0:T(2,128)(2,1)} %reshape.910), calls=%async_computation | async-start | bytes 1048576 | tf_op jit(solution)/shard_map/all_to_all | solution.py:176
  51.0 21.4 %all-to-all-done = bf16[64,2,2048]{2,1,0:T(2,128)(2,1)S(1)} async-done(((bf16[64,2,2048]{2,1,0:T(2,128)(2,1)}), bf16[64,2,2048]{2,1,0:T(2,128)(2,1)S(1)}, u32[]{:S(2)}, u32[]{:S(2)}) %all-to-all-start) | async-done | bytes 524320 | tf_op jit(solution)/shard_map/all_to_all | solution.py:176
  72.4 4.1 reshape.911
  76.5 8.2 %copy.195 = bf16[2,16,64,128]{3,1,2,0:T(8,128)(2,1)S(1)} copy(bf16[2,16,64,128]{1,0,3,2:T(2,128)(2,1)} %bitcast.209) | data formatting | bytes 1048576 | tf_op jit(solution)/shard_map/all_to_all | solution.py:176
  85.4 0.9 pad_maximum_fusion.7
  86.3 0.6 fusion.150
  89.2 0.6 gather_fusion
  90.3 105.2 %all-gather.2.cloned.1.call-done = bf16[2,64,128,128]{3,2,1,0:T(8,128)(2,1)} async-done(((bf16[2,8,128,128]{3,2,1,0:T(8,128)(2,1)}), bf16[2,64,128,128]{3,2,1,0:T(8,128)(2,1)}) %all-gather.2.cloned.1.call-update) | async-done | bytes 4194320 | tf_op jit(solution)/shard_map/all_gather | solution.py:196
  195.5 7.0 cosine_convert_fusion
  203.3 0.5 convolution_bitcast_fusion.5
  203.7 0.7 subtract_convert_fusion.5
  204.5 0.9 convolution_bitcast_fusion.4
  205.4 0.7 subtract_convert_fusion.4
  206.2 0.5 convolution_bitcast_fusion.3
  206.6 1.2 copy.262
  207.8 0.7 subtract_convert_fusion.3
  208.6 0.5 fusion.3
  209.1 1.7 copy.157
  210.7 11.7 %all-to-all-start.1 = ((bf16[2,64,32,128]{3,2,0,1:T(8,128)(2,1)}), bf16[2,64,32,128]{3,2,0,1:T(8,128)(2,1)S(1)}, u32[]{:S(2)}, u32[]{:S(2)}) async-start(bf16[2,64,32,128]{3,2,0,1:T(8,128)(2,1)} %copy.157), calls=%async_computation.1 | async-start | bytes 2097152 | tf_op jit(solution)/shard_map/all_to_all | solution.py:201
  223.8 53.2 %all-to-all-done.1 = bf16[2,64,32,128]{3,2,0,1:T(8,128)(2,1)S(1)} async-done(((bf16[2,64,32,128]{3,2,0,1:T(8,128)(2,1)}), bf16[2,64,32,128]{3,2,0,1:T(8,128)(2,1)S(1)}, u32[]{:S(2)}, u32[]{:S(2)}) %all-to-all-start.1) | async-done | bytes 1048608 | tf_op jit(solution)/shard_map/all_to_all | solution.py:201
  277.0 0.9 convolution_bitcast_fusion.2
  279.0 0.5 convolution_bitcast_fusion
  279.8 0.5 fusion.2
  280.8 1.1 fusion.149
  282.4 32.9 %gather_fusion.1 = f32[8192]{0:T(1024)S(1)} fusion(f32[1024]{0:T(1024)S(1)} %multiply_bitcast_fusion, s32[8192]{0:T(1024)S(1)} %broadcast_clamp_fusion), kind=kCustom, calls=%fused_computation.1 | custom fusion | bytes 98304 | tf_op jit(solution)/shard_map/jit(_take)/gather | solution.py:218
  315.3 0.6 broadcast_select_fusion.1
  316.0 0.6 broadcast_select_fusion
  316.6 442.6 %all-reduce.3.cloned.1.call-done = (f32[8192]{0:T(1024)}, f32[8192]{0:T(1024)}) async-done(((f32[8192]{0:T(1024)}, f32[8192]{0:T(1024)}), (f32[8192]{0:T(1024)}, f32[8192]{0:T(1024)})) %all-reduce.3.cloned.1.call-update) | async-done | bytes 65552 | tf_op jit(solution)/shard_map/psum | solution.py:224
  759.2 1.3 log_multiply_fusion
  (66 shorter events, 7.9 us)
Async XLA Ops:
  28.3 44.1 %all-to-all-start = ((bf16[64,2,2048]{2,1,0:T(2,128)(2,1)}), bf16[64,2,2048]{2,1,0:T(2,128)(2,1)S(1)}, u32[]{:S(2)}, u32[]{:S(2)}) async-start(bf16[64,2,2048]{2,1,0:T(2,128)(2,1)} %reshape.910), calls=%async_computation | async-start | bytes 1048576 | tf_op jit(solution)/shard_map/all_to_all | solution.py:176
  50.5 144.9 %all-gather.2.cloned.1.call-start = ((), (), s32[]{:S(2)}) async-start(), calls=%async_computation.2 | async-start | bytes 4718592 | tf_op jit(solution)/shard_map/all_gather | solution.py:196
  84.7 1.5 copy-start.4
  209.0 14.5 %copy-start = (s32[1,8192]{1,0:T(1,128)S(1)}, s32[1,8192]{1,0:T(1,128)}, u32[]{:S(2)}) copy-start(s32[1,8192]{1,0:T(1,128)} %param.9) | copy-start | bytes 98308
  210.7 66.3 %all-to-all-start.1 = ((bf16[2,64,32,128]{3,2,0,1:T(8,128)(2,1)}), bf16[2,64,32,128]{3,2,0,1:T(8,128)(2,1)S(1)}, u32[]{:S(2)}, u32[]{:S(2)}) async-start(bf16[2,64,32,128]{3,2,0,1:T(8,128)(2,1)} %copy.157), calls=%async_computation.1 | async-start | bytes 2097152 | tf_op jit(solution)/shard_map/all_to_all | solution.py:201
  222.4 536.8 %all-reduce.3.cloned.1.call-start = ((), (), s32[]{:S(2)}) async-start(), calls=%async_computation.3 | async-start | bytes 131072 | tf_op jit(solution)/shard_map/psum | solution.py:224
  282.4 32.9 %copy-start.3 = (f32[8,128]{1,0:T(8,128)}, f32[8,128]{1,0:T(8,128)S(1)}, u32[]{:S(2)}) copy-start(f32[8,128]{1,0:T(8,128)S(1)} %fusion.13) | copy-start | bytes 12292
  282.4 32.9 %copy-start.1 = (f32[1,8192]{1,0:T(1,128)S(1)}, f32[1,8192]{1,0:T(1,128)}, u32[]{:S(2)}) copy-start(f32[1,8192]{1,0:T(1,128)} %param.10) | copy-start | bytes 98308
  282.4 32.9 %copy-start.2 = (s32[8192]{0:T(1024)S(1)}, s32[8192]{0:T(1024)}, u32[]{:S(2)}) copy-start(s32[8192]{0:T(1024)} %param.11) | copy-start | bytes 98308
Sparse Core Ops, SparseCore 0:
  86.4 109.0 all-gather.1
  316.7 442.4 all-reduce.2
where the time goes:
time: 768 us; the launch traced here: 767 us
  waiting for transfers between devices  623 us (81%)
  local copies, waits for them, and re-layouts  68.2 us (9%)
  starting transfers between devices  34.4 us (4%)
  between operations  17.2 us (2%)
  matrix products  12.9 us (2%)
  other arithmetic  12.1 us (2%)
    psum x1, waiting for transfers between devices, body(): lax.psum((signal_part, interference_part), ('dir', 'row'))  443 us
    all_gather x1, waiting for transfers between devices, body(): lax.all_gather(section_one, 'dir', axis=1, tiled=True)  105 us
    all_to_all x1, waiting for transfers between devices, body(): lax.all_to_all(stacked_field, 'row', split_axis=1, concat_axis=3, tiled=T...  53.2 us
    gather x1, local copies, waits for them, and re-layouts, body(): jnp.take(faded_flat, jnp.clip(local_tile, 0, tile_total - 1))  32.9 us
    all_to_all x1, starting transfers between devices, body(): lax.all_to_all(half_screen, 'row', split_axis=2, concat_axis=1, tiled=True)  22.2 us
    all_to_all x1, waiting for transfers between devices, body(): lax.all_to_all(half_screen, 'row', split_axis=2, concat_axis=1, tiled=True)  21.4 us
    unnamed x13, local copies, waits for them, and re-layouts  17.1 us
  transfers between devices with their start and end apart: 4, of which 4 were waited for; matrix products, arithmetic and copies ran while one was open for 0% of the time, Pallas kernels for 0%

commit v1 on v0

--- a/solution.py
+++ b/solution.py
@@ -211,21 +211,29 @@
     first_moment = jnp.sum(tile_one.reshape(YTILES, tile_rows, XTILES), axis=1)
     second_moment = jnp.sum(tile_two.reshape(YTILES, tile_rows, XTILES), axis=1)
     fluctuation, faded_power = tile_statistics(first_moment, second_moment, window[0], tile_rows)
-    faded_flat = faded_power.reshape(-1)
-    tile_total = faded_flat.shape[0]
+    tile_total = faded_power.shape[0] * faded_power.shape[1]
     local_tile = tile_map[0] - lax.axis_index("row") * tile_total
     inside = (local_tile >= 0) & (local_tile < tile_total)
-    looked = jnp.where(inside, jnp.take(faded_flat, jnp.clip(local_tile, 0, tile_total - 1)), 0.0)
+    tile_row = local_tile // XTILES
+    tile_column = local_tile % XTILES
+    pick_row = (tile_row[:, None] == jnp.arange(YTILES, dtype=jnp.int32)[None, :]).astype(jnp.float32)
+    row_values = jnp.dot(pick_row, faded_power, precision=lax.Precision.HIGHEST)
+    pick_column = tile_column[:, None] == jnp.arange(XTILES, dtype=jnp.int32)[None, :]
+    looked = jnp.sum(jnp.where(pick_column, row_values, 0.0), axis=1)
+    looked = jnp.where(inside, looked, 0.0)
     received = link_gain[0] * looked
     direction = lax.axis_index("dir")
     serves_here = serving == direction
     signal_part = jnp.where(serves_here, received, 0.0)
     interference_part = jnp.where(serves_here, 0.0, received)
-    signal, interference = lax.psum((signal_part, interference_part), ("dir", "row"))
-    share_size = serving.shape[0] // lax.axis_size(("dir", "row"))
-    share_start = lax.axis_index(("dir", "row")) * share_size
-    signal = lax.dynamic_slice_in_dim(signal, share_start, share_size, 0)
-    interference = lax.dynamic_slice_in_dim(interference, share_start, share_size, 0)
+    dir_count = lax.axis_size("dir")
+    share_size = serving.shape[0] // (dir_count * row_count)
+    parts = jnp.stack([signal_part, interference_part]).reshape(2, dir_count, row_count, share_size)
+    parts = lax.all_to_all(parts, "row", split_axis=2, concat_axis=2, tiled=True)
+    parts = jnp.sum(parts, axis=2, keepdims=True)
+    parts = lax.all_to_all(parts, "dir", split_axis=1, concat_axis=1, tiled=True)
+    parts = jnp.sum(parts, axis=(1, 2))
+    signal, interference = parts[0], parts[1]
     signal_ratio = jnp.log10(signal / (interference + noise_floor))
     return (fluctuation[None], signal_ratio)
 

time: 768 us -> 337 us (0.44)
  waiting for transfers between devices: 623 us -> 180 us
  blocking collectives: 0 us -> 42.1 us
  local copies, waits for them, and re-layouts: 68.2 us -> 36.8 us
    psum x1 -> x0, waiting for transfers between devices: 443 us -> none  [body(): lax.psum((signal_part, interference_part), ('dir', 'row'))]
    all_to_all x0 -> x2, blocking collectives: none -> 42.1 us  [the longest x1 22.5 us: body(): lax.all_to_all(parts, 'dir', split_axis=1, concat_axis=1, tiled=True)]
    gather x1 -> x0, local copies, waits for them, and re-layouts: 32.9 us -> none  [body(): jnp.take(faded_flat, jnp.clip(local_tile, 0, tile_total - 1))]
    unnamed x13 -> x15, local copies, waits for them, and re-layouts: 17.1 us -> 17.5 us
  transfers between devices with their start and end apart: 4 -> 3, of which waited for: 4 -> 3; matrix products, arithmetic and copies ran while one was open for 0% -> 1% of each run, Pallas kernels for 0% -> 0%
where the time goes in v1:
time: 337 us
  waiting for transfers between devices  180 us (53%)
  blocking collectives  42.1 us (12%)
  local copies, waits for them, and re-layouts  36.8 us (11%)
  starting transfers between devices  34.2 us (10%)
  between operations  17.2 us (5%)
  matrix products  15.2 us (5%)
  other arithmetic  10.9 us (3%)
    all_gather x1, waiting for transfers between devices, body(): lax.all_gather(section_one, 'dir', axis=1, tiled=True)  105 us
    all_to_all x1, waiting for transfers between devices, body(): lax.all_to_all(stacked_field, 'row', split_axis=1, concat_axis=3, tiled=T...  53.6 us
    all_to_all x1, blocking collectives, body(): lax.all_to_all(parts, 'dir', split_axis=1, concat_axis=1, tiled=True)  22.5 us
    all_to_all x1, starting transfers between devices, body(): lax.all_to_all(half_screen, 'row', split_axis=2, concat_axis=1, tiled=True)  22.2 us
    all_to_all x1, waiting for transfers between devices, body(): lax.all_to_all(half_screen, 'row', split_axis=2, concat_axis=1, tiled=True)  21.4 us
    all_to_all x1, blocking collectives, body(): lax.all_to_all(parts, 'row', split_axis=2, concat_axis=2, tiled=True)  19.7 us
    unnamed x15, local copies, waits for them, and re-layouts  17.5 us
    dot_general x12, matrix products, contract(): jnp.einsum(pattern, operand, matrix, preferred_element_type=jnp.float32)  12.6 us
  transfers between devices with their start and end apart: 3, of which 3 were waited for; matrix products, arithmetic and copies ran while one was open for 1% of the time, Pallas kernels for 0%

profile of v1, /device:TPU:1, one launch (start us, length us, event | category | flops | bytes accessed | tf_op | source)
XLA Modules:
  0.0 336.6 jit_solution(16652421525079852267)
XLA Ops:
  8.5 1.1 multiply_convert_fusion
  10.7 4.7 %copy.233 = bf16[2,16,64,128]{1,0,3,2:T(2,128)(2,1)} copy(bf16[2,16,64,128]{3,2,1,0:T(8,128)(2,1)S(1)} %fusion.13) | data formatting | bytes 1048576 | tf_op jit(solution)/shard_map/reshape | solution.py:175
  15.4 12.9 %reshape.901 = bf16[64,2,2048]{2,1,0:T(2,128)(2,1)} reshape(bf16[8192,2,16]{2,1,0:T(2,128)(2,1)} %bitcast.211) | data formatting | bytes 1048576
  28.3 22.2 %all-to-all-start = ((bf16[64,2,2048]{2,1,0:T(2,128)(2,1)}), bf16[64,2,2048]{2,1,0:T(2,128)(2,1)S(1)}, u32[]{:S(2)}, u32[]{:S(2)}) async-start(bf16[64,2,2048]{2,1,0:T(2,128)(2,1)} %reshape.901), calls=%async_computation | async-start | bytes 1048576 | tf_op jit(solution)/shard_map/all_to_all | solution.py:176
  50.9 21.4 %all-to-all-done = bf16[64,2,2048]{2,1,0:T(2,128)(2,1)S(1)} async-done(((bf16[64,2,2048]{2,1,0:T(2,128)(2,1)}), bf16[64,2,2048]{2,1,0:T(2,128)(2,1)S(1)}, u32[]{:S(2)}, u32[]{:S(2)}) %all-to-all-start) | async-done | bytes 524320 | tf_op jit(solution)/shard_map/all_to_all | solution.py:176
  72.3 4.1 %reshape.902 = bf16[8192,2,16]{2,1,0:T(2,128)(2,1)} reshape(bf16[64,2,2048]{2,1,0:T(2,128)(2,1)S(1)} %all-to-all-done) | data formatting | bytes 1048576
  76.4 8.2 %copy.235 = bf16[2,16,64,128]{3,1,2,0:T(8,128)(2,1)S(1)} copy(bf16[2,16,64,128]{1,0,3,2:T(2,128)(2,1)} %bitcast.212) | data formatting | bytes 1048576 | tf_op jit(solution)/shard_map/all_to_all | solution.py:176
  85.3 0.8 pad_maximum_fusion.7
  86.2 0.6 fusion.157
  89.1 0.6 gather_fusion
  90.2 105.3 %all-gather.2.cloned.1.call-done = bf16[2,64,128,128]{3,2,1,0:T(8,128)(2,1)} async-done(((bf16[2,8,128,128]{3,2,1,0:T(8,128)(2,1)}), bf16[2,64,128,128]{3,2,1,0:T(8,128)(2,1)}) %all-gather.2.cloned.1.call-update) | async-done | bytes 4194320 | tf_op jit(solution)/shard_map/all_gather | solution.py:196
  195.5 7.0 %cosine_convert_fusion = (bf16[16,128,128]{2,0,1:T(8,128)(2,1)S(1)}, bf16[16,128,128]{2,0,1:T(8,128)(2,1)S(1)}) fusion(f32[]{:T(128)} %bitcast.44, bf16[2,64,128,128]{3,2,1,0:T(8,128)(2,1)} %all-gather.2.cloned.1.call-done, bf16[2,16,64]{2,0,1:T(2,128)(2,1)S(1)} %fusion.132), kind=kOutput, calls=%fused_computation.68 | convolution fusion | flops 67895296 | bytes 5246980 | tf_op jit(solution)/shard_map/zkbx,zak->abx/dot_general | solution.py:98
  203.2 0.5 convolution_bitcast_fusion.5
  203.7 0.7 subtract_convert_fusion.5
  204.5 0.9 convolution_bitcast_fusion.4
  205.4 0.7 subtract_convert_fusion.4
  206.6 1.2 copy.303
  207.8 0.7 subtract_convert_fusion.3
  208.5 0.5 fusion.3
  209.0 1.6 copy.195
  210.7 11.7 %all-to-all-start.1 = ((bf16[2,64,32,128]{3,2,0,1:T(8,128)(2,1)}), bf16[2,64,32,128]{3,2,0,1:T(8,128)(2,1)S(1)}, u32[]{:S(2)}, u32[]{:S(2)}) async-start(bf16[2,64,32,128]{3,2,0,1:T(8,128)(2,1)} %copy.195), calls=%async_computation.1 | async-start | bytes 2097152 | tf_op jit(solution)/shard_map/all_to_all | solution.py:201
  223.3 53.6 %all-to-all-done.1 = bf16[2,64,32,128]{3,2,0,1:T(8,128)(2,1)S(1)} async-done(((bf16[2,64,32,128]{3,2,0,1:T(8,128)(2,1)}), bf16[2,64,32,128]{3,2,0,1:T(8,128)(2,1)S(1)}, u32[]{:S(2)}, u32[]{:S(2)}) %all-to-all-start.1) | async-done | bytes 1048608 | tf_op jit(solution)/shard_map/all_to_all | solution.py:201
  276.9 0.9 convolution_bitcast_fusion.2
  278.9 0.5 convolution_bitcast_fusion
  279.6 0.5 fusion.2
  280.7 1.1 fusion.156
  282.2 2.3 fusion.4
  285.4 19.7 %all_to_all.40 = f32[64,1,256]{2,1,0:T(1,128)S(1)} all-to-all(f32[64,1,256]{2,1,0:T(1,128)S(1)} %reshape.903), channel_id=1, replica_groups=mesh['dir'=8,'row'=64] {'row'}, dimensions={0} | all-to-all | bytes 131072 | tf_op jit(solution)/shard_map/all_to_all | solution.py:232
  305.1 0.5 broadcast.1339
  305.6 0.8 reduce
  306.7 22.5 %all_to_all.41 = f32[2,8,1,16]{3,0,2,1:T(2,128)S(1)} all-to-all(f32[2,8,1,16]{3,0,2,1:T(2,128)S(1)} %copy.205), channel_id=1, replica_groups=mesh['dir'=8,'row'=64] {'dir'}, dimensions={1} | all-to-all | bytes 2048 | tf_op jit(solution)/shard_map/all_to_all | solution.py:234
  329.2 0.5 multiply_bitcast_fusion
  (74 shorter events, 9.1 us)
Async XLA Ops:
  28.3 44.0 %all-to-all-start = ((bf16[64,2,2048]{2,1,0:T(2,128)(2,1)}), bf16[64,2,2048]{2,1,0:T(2,128)(2,1)S(1)}, u32[]{:S(2)}, u32[]{:S(2)}) async-start(bf16[64,2,2048]{2,1,0:T(2,128)(2,1)} %reshape.901), calls=%async_computation | async-start | bytes 1048576 | tf_op jit(solution)/shard_map/all_to_all | solution.py:176
  50.5 145.0 %all-gather.2.cloned.1.call-start = ((), (), s32[]{:S(2)}) async-start(), calls=%async_computation.4 | async-start | bytes 4718592 | tf_op jit(solution)/shard_map/all_gather | solution.py:196
  84.6 1.5 copy-start.3
  209.0 14.2 %copy-start.1 = (s32[1,8192]{1,0:T(1,128)S(1)}, s32[1,8192]{1,0:T(1,128)}, u32[]{:S(2)}) copy-start(s32[1,8192]{1,0:T(1,128)} %param.9) | copy-start | bytes 98308
  210.7 66.2 %all-to-all-start.1 = ((bf16[2,64,32,128]{3,2,0,1:T(8,128)(2,1)}), bf16[2,64,32,128]{3,2,0,1:T(8,128)(2,1)S(1)}, u32[]{:S(2)}, u32[]{:S(2)}) async-start(bf16[2,64,32,128]{3,2,0,1:T(8,128)(2,1)} %copy.195), calls=%async_computation.1 | async-start | bytes 2097152 | tf_op jit(solution)/shard_map/all_to_all | solution.py:201
  282.1 2.5 copy-start
  282.1 2.5 copy-start.2
  282.2 2.3 copy-start.4
Sparse Core Ops, SparseCore 0:
  86.3 109.1 all-gather.1

commit v2 on v1

--- a/solution.py
+++ b/solution.py
@@ -169,24 +169,26 @@
     column_ids = jnp.arange(N, dtype=jnp.int32)
     spectral_gain = spectral_filter(row_ids, column_ids)
     spectrum = (white_noise.astype(jnp.float32) * spectral_gain).astype(jnp.bfloat16)
-    half_screen = inverse_axis(
+    section_first = inverse_first(
         spectrum.reshape(2, rows_here, FIRST, SECOND), tables, row_patterns, False
     )
-    half_screen = half_screen.astype(jnp.bfloat16).reshape(2, rows_here, N)
-    turned = lax.all_to_all(half_screen, "row", split_axis=2, concat_axis=1, tiled=True)
-    band_rows = turned.shape[1]
-    columns = turned.shape[2]
+    half_screen = contract("zrkb,wzak->awrb", section_first, tables[0]) * (1.0 / N)
+    half_screen = half_screen.astype(jnp.bfloat16)
+    turned = lax.all_to_all(half_screen, "row", split_axis=0, concat_axis=0, tiled=True)
     slant_factor = 1.0 + 0.25 * geometry[0, 1].astype(jnp.float32)
     fresnel_x = fresnel_factor(geometry[0], FIRST, SECOND)
     fresnel_y = fresnel_factor(geometry[0], row_count, ROWS_DEV)
     offset_rows = N // 4 * geometry[0, 1]
-    blocks = band_rows // SECOND
+    columns = SECOND
+    blocks = row_count * rows_here // SECOND
+    split = SECOND // rows_here
     block_start = lax.axis_index("dir") * blocks
-    stacked = turned.reshape(2, blocks, SECOND, columns)
+    stacked = turned.reshape(blocks, split, 2, rows_here, columns)
+    inner_split = tables[1].reshape(2, 2, SECOND, split, rows_here)
     twist_real = lax.dynamic_slice_in_dim(tables[2], block_start, blocks, 0)[..., None]
     twist_imag = lax.dynamic_slice_in_dim(tables[3], block_start, blocks, 0)[..., None]
     section_one = complex_times(
-        contract("zkcx,wzbc->wkbx", stacked, tables[1]), twist_real, -twist_imag
+        contract("khzrx,wzbhr->wkbx", stacked, inner_split), twist_real, -twist_imag
     )
     section_one = section_one.astype(jnp.bfloat16)
     outer_count = patch_len // SECOND

time: 337 us -> 308 us (0.914)
  local copies, waits for them, and re-layouts: 36.8 us -> 8.04 us
    unnamed x15 -> x13, local copies, waits for them, and re-layouts: 17.5 us -> 0.55 us
    all_to_all x1 -> x0, local copies, waits for them, and re-layouts: 8.21 us -> none  [body(): lax.all_to_all(half_screen, 'row', split_axis=2, concat_axis=1, tiled=True)]
    reshape x1 -> x0, local copies, waits for them, and re-layouts: 4.72 us -> none  [body(): half_screen = half_screen.astype(jnp.bfloat16).reshape(2, rows_here, N)]
where the time goes in v2:
time: 308 us
  waiting for transfers between devices  180 us (58%)
  blocking collectives  42.1 us (14%)
  starting transfers between devices  34.2 us (11%)
  between operations  17.2 us (6%)
  matrix products  15.2 us (5%)
  other arithmetic  11.2 us (4%)
  local copies, waits for them, and re-layouts  8.04 us (3%)
    all_gather x1, waiting for transfers between devices, body(): lax.all_gather(section_one, 'dir', axis=1, tiled=True)  105 us
    all_to_all x1, waiting for transfers between devices, body(): lax.all_to_all(stacked_field, 'row', split_axis=1, concat_axis=3, tiled=T...  53.6 us
    all_to_all x1, blocking collectives, body(): lax.all_to_all(parts, 'dir', split_axis=1, concat_axis=1, tiled=True)  22.4 us
    all_to_all x1, starting transfers between devices, body(): lax.all_to_all(half_screen, 'row', split_axis=0, concat_axis=0, tiled=True)  22.2 us
    all_to_all x1, waiting for transfers between devices, body(): lax.all_to_all(half_screen, 'row', split_axis=0, concat_axis=0, tiled=True)  21.1 us
    all_to_all x1, blocking collectives, body(): lax.all_to_all(parts, 'row', split_axis=2, concat_axis=2, tiled=True)  19.7 us
    dot_general x12, matrix products, contract(): jnp.einsum(pattern, operand, matrix, preferred_element_type=jnp.float32)  12.6 us
    all_to_all x1, starting transfers between devices, body(): lax.all_to_all(stacked_field, 'row', split_axis=1, concat_axis=3, tiled=T...  11.7 us
  transfers between devices with their start and end apart: 3, of which 3 were waited for; matrix products, arithmetic and copies ran while one was open for 1% of the time, Pallas kernels for 0%

profile of v2, /device:TPU:1, one launch (start us, length us, event | category | flops | bytes accessed | tf_op | source)
XLA Modules:
  0.0 307.8 jit_solution(7928086707628015967)
XLA Ops:
  8.5 1.1 multiply_convert_fusion
  10.7 1.1 copy.143
  11.8 22.2 %all-to-all-start = ((bf16[64,2,16,128]{3,2,1,0:T(8,128)(2,1)}), bf16[64,2,16,128]{3,2,1,0:T(8,128)(2,1)S(1)}, u32[]{:S(2)}, u32[]{:S(2)}) async-start(bf16[64,2,16,128]{3,2,1,0:T(8,128)(2,1)} %copy.143), calls=%async_computation | async-start | bytes 1048576 | tf_op jit(solution)/shard_map/all_to_all | solution.py:177
  34.5 0.3 negate_convert_fusion
  34.8 21.1 %all-to-all-done = bf16[64,2,16,128]{3,2,1,0:T(8,128)(2,1)S(1)} async-done(((bf16[64,2,16,128]{3,2,1,0:T(8,128)(2,1)}), bf16[64,2,16,128]{3,2,1,0:T(8,128)(2,1)S(1)}, u32[]{:S(2)}, u32[]{:S(2)}) %all-to-all-start) | async-done | bytes 524320 | tf_op jit(solution)/shard_map/all_to_all | solution.py:177
  56.6 0.8 pad_maximum_fusion.7
  57.5 0.6 fusion.171
  60.4 0.6 gather_fusion
  61.5 105.2 %all-gather.2.cloned.1.call-done = bf16[2,64,128,128]{3,2,1,0:T(8,128)(2,1)} async-done(((bf16[2,8,128,128]{3,2,1,0:T(8,128)(2,1)}), bf16[2,64,128,128]{3,2,1,0:T(8,128)(2,1)}) %all-gather.2.cloned.1.call-update) | async-done | bytes 4194320 | tf_op jit(solution)/shard_map/all_gather | solution.py:198
  166.7 7.0 %cosine_convert_fusion = (bf16[16,128,128]{2,0,1:T(8,128)(2,1)S(1)}, bf16[16,128,128]{2,0,1:T(8,128)(2,1)S(1)}) fusion(f32[]{:T(128)} %bitcast.43, bf16[2,64,128,128]{3,2,1,0:T(8,128)(2,1)} %all-gather.2.cloned.1.call-done, bf16[2,16,64]{2,0,1:T(2,128)(2,1)S(1)} %fusion.144), kind=kOutput, calls=%fused_computation.68 | convolution fusion | flops 67895296 | bytes 5246980 | tf_op jit(solution)/shard_map/zkbx,zak->abx/dot_general | solution.py:98
  174.5 0.5 convolution_bitcast_fusion.5
  174.9 0.7 subtract_convert_fusion.5
  175.7 0.9 convolution_bitcast_fusion.4
  176.6 0.7 subtract_convert_fusion.4
  177.3 0.5 convolution_bitcast_fusion.3
  177.8 1.2 copy.260
  179.0 0.7 subtract_convert_fusion.3
  179.7 0.5 fusion.3
  180.2 1.7 copy.158
  181.9 11.7 %all-to-all-start.1 = ((bf16[2,64,32,128]{3,2,0,1:T(8,128)(2,1)}), bf16[2,64,32,128]{3,2,0,1:T(8,128)(2,1)S(1)}, u32[]{:S(2)}, u32[]{:S(2)}) async-start(bf16[2,64,32,128]{3,2,0,1:T(8,128)(2,1)} %copy.158), calls=%async_computation.1 | async-start | bytes 2097152 | tf_op jit(solution)/shard_map/all_to_all | solution.py:203
  194.6 53.6 %all-to-all-done.1 = bf16[2,64,32,128]{3,2,0,1:T(8,128)(2,1)S(1)} async-done(((bf16[2,64,32,128]{3,2,0,1:T(8,128)(2,1)}), bf16[2,64,32,128]{3,2,0,1:T(8,128)(2,1)S(1)}, u32[]{:S(2)}, u32[]{:S(2)}) %all-to-all-start.1) | async-done | bytes 1048608 | tf_op jit(solution)/shard_map/all_to_all | solution.py:203
  248.1 0.9 convolution_bitcast_fusion.2
  249.3 0.4 convolution_bitcast_fusion.1
  250.1 0.5 convolution_bitcast_fusion
  250.9 0.5 fusion.2
  251.9 1.1 fusion.170
  253.5 2.3 fusion.4
  256.7 19.7 %all_to_all.30 = f32[64,1,256]{2,1,0:T(1,128)S(1)} all-to-all(f32[64,1,256]{2,1,0:T(1,128)S(1)} %reshape.950), channel_id=1, replica_groups=mesh['dir'=8,'row'=64] {'row'}, dimensions={0} | all-to-all | bytes 131072 | tf_op jit(solution)/shard_map/all_to_all | solution.py:234
  276.3 0.5 broadcast.1443
  276.9 0.8 reduce
  278.0 22.4 %all_to_all.31 = f32[2,8,1,16]{3,0,2,1:T(2,128)S(1)} all-to-all(f32[2,8,1,16]{3,0,2,1:T(2,128)S(1)} %copy.168), channel_id=1, replica_groups=mesh['dir'=8,'row'=64] {'dir'}, dimensions={1} | all-to-all | bytes 2048 | tf_op jit(solution)/shard_map/all_to_all | solution.py:236
  300.4 0.5 multiply_bitcast_fusion
  (73 shorter events, 8.2 us)
Async XLA Ops:
  11.8 44.1 %all-to-all-start = ((bf16[64,2,16,128]{3,2,1,0:T(8,128)(2,1)}), bf16[64,2,16,128]{3,2,1,0:T(8,128)(2,1)S(1)}, u32[]{:S(2)}, u32[]{:S(2)}) async-start(bf16[64,2,16,128]{3,2,1,0:T(8,128)(2,1)} %copy.143), calls=%async_computation | async-start | bytes 1048576 | tf_op jit(solution)/shard_map/all_to_all | solution.py:177
  34.1 132.6 %all-gather.2.cloned.1.call-start = ((), (), s32[]{:S(2)}) async-start(), calls=%async_computation.4 | async-start | bytes 4718592 | tf_op jit(solution)/shard_map/all_gather | solution.py:198
  55.9 1.5 copy-start.3
  180.2 14.3 %copy-start.1 = (s32[1,8192]{1,0:T(1,128)S(1)}, s32[1,8192]{1,0:T(1,128)}, u32[]{:S(2)}) copy-start(s32[1,8192]{1,0:T(1,128)} %param.9) | copy-start | bytes 98308
  181.9 66.2 %all-to-all-start.1 = ((bf16[2,64,32,128]{3,2,0,1:T(8,128)(2,1)}), bf16[2,64,32,128]{3,2,0,1:T(8,128)(2,1)S(1)}, u32[]{:S(2)}, u32[]{:S(2)}) async-start(bf16[2,64,32,128]{3,2,0,1:T(8,128)(2,1)} %copy.158), calls=%async_computation.1 | async-start | bytes 2097152 | tf_op jit(solution)/shard_map/all_to_all | solution.py:203
  253.3 2.5 copy-start
  253.3 2.5 copy-start.2
  253.5 2.3 copy-start.4
Sparse Core Ops, SparseCore 0:
  57.6 109.0 all-gather.1

commit v3 on v2

--- a/solution.py
+++ b/solution.py
@@ -158,6 +158,34 @@
     return result.astype(jnp.bfloat16).reshape(2, patch_rows, width_here)
 
 
+def column_front(chunk, tables, row_count, rows_here):
+    turned = lax.all_to_all(chunk, "row", split_axis=0, concat_axis=0, tiled=True)
+    columns = chunk.shape[-1]
+    blocks = row_count * rows_here // SECOND
+    split = SECOND // rows_here
+    block_start = lax.axis_index("dir") * blocks
+    stacked = turned.reshape(blocks, split, 2, rows_here, columns)
+    inner_split = tables[1].reshape(2, 2, SECOND, split, rows_here)
+    twist_real = lax.dynamic_slice_in_dim(tables[2], block_start, blocks, 0)[..., None]
+    twist_imag = lax.dynamic_slice_in_dim(tables[3], block_start, blocks, 0)[..., None]
+    section_one = complex_times(
+        contract("khzrx,wzbhr->wkbx", stacked, inner_split), twist_real, -twist_imag
+    )
+    return section_one.astype(jnp.bfloat16)
+
+
+def column_tail(gathered, tables, tables_y, slant_factor, fresnel_y, offset_rows, patch_len, row_count):
+    columns = gathered.shape[-1]
+    outer_count = patch_len // SECOND
+    outer_ids = (offset_rows // SECOND + jnp.arange(outer_count, dtype=jnp.int32)) % FIRST
+    patch_outer = jnp.take(tables[0][0], outer_ids, axis=1)
+    phase_patch = contract("zkbx,zak->abx", gathered, patch_outer)
+    phase_patch = phase_patch.reshape(patch_len, columns) * (1.0 / N)
+    screen_field = propagate_columns(phase_patch, tables_y, slant_factor, fresnel_y)
+    stacked_field = screen_field.reshape(2, row_count, ROWS_DEV, columns)
+    return lax.all_to_all(stacked_field, "row", split_axis=1, concat_axis=3, tiled=True)
+
+
 def body(white_noise, geometry, window, tile_map, link_gain, serving):
     row_count = lax.axis_size("row")
     tables = transform_tables(FIRST, SECOND)
@@ -174,33 +202,31 @@
     )
     half_screen = contract("zrkb,wzak->awrb", section_first, tables[0]) * (1.0 / N)
     half_screen = half_screen.astype(jnp.bfloat16)
-    turned = lax.all_to_all(half_screen, "row", split_axis=0, concat_axis=0, tiled=True)
     slant_factor = 1.0 + 0.25 * geometry[0, 1].astype(jnp.float32)
     fresnel_x = fresnel_factor(geometry[0], FIRST, SECOND)
     fresnel_y = fresnel_factor(geometry[0], row_count, ROWS_DEV)
     offset_rows = N // 4 * geometry[0, 1]
-    columns = SECOND
-    blocks = row_count * rows_here // SECOND
-    split = SECOND // rows_here
-    block_start = lax.axis_index("dir") * blocks
-    stacked = turned.reshape(blocks, split, 2, rows_here, columns)
-    inner_split = tables[1].reshape(2, 2, SECOND, split, rows_here)
-    twist_real = lax.dynamic_slice_in_dim(tables[2], block_start, blocks, 0)[..., None]
-    twist_imag = lax.dynamic_slice_in_dim(tables[3], block_start, blocks, 0)[..., None]
-    section_one = complex_times(
-        contract("khzrx,wzbhr->wkbx", stacked, inner_split), twist_real, -twist_imag
-    )
-    section_one = section_one.astype(jnp.bfloat16)
-    outer_count = patch_len // SECOND
-    outer_ids = (offset_rows // SECOND + jnp.arange(outer_count, dtype=jnp.int32)) % FIRST
-    patch_outer = jnp.take(tables[0][0], outer_ids, axis=1)
-    phase_patch = contract(
-        "zkbx,zak->abx", lax.all_gather(section_one, "dir", axis=1, tiled=True), patch_outer
-    )
-    phase_patch = phase_patch.reshape(patch_len, columns) * (1.0 / N)
-    screen_field = propagate_columns(phase_patch, tables_y, slant_factor, fresnel_y)
-    stacked_field = screen_field.reshape(2, row_count, ROWS_DEV, columns)
-    portion = lax.all_to_all(stacked_field, "row", split_axis=1, concat_axis=3, tiled=True)
+    pieces = 2
+    piece_width = SECOND // pieces
+    portions = []
+    previous = None
+    for piece in range(pieces):
+        chunk = half_screen[..., piece * piece_width : (piece + 1) * piece_width]
+        if previous is not None:
+            previous, chunk = lax.optimization_barrier((previous, chunk))
+        section_one = column_front(chunk, tables, row_count, rows_here)
+        gathered = lax.all_gather(section_one, "dir", axis=1, tiled=True)
+        if portions:
+            portions[-1], gathered = lax.optimization_barrier((portions[-1], gathered))
+        portions.append(
+            column_tail(
+                gathered, tables, tables_y, slant_factor, fresnel_y, offset_rows, patch_len, row_count
+            )
+        )
+        previous = section_one
+    portion = jnp.stack(
+        [p.reshape(2, ROWS_DEV, row_count, piece_width) for p in portions], axis=3
+    ).reshape(2, 1, ROWS_DEV, N)
     item_count = portion.shape[2]
     stacked = portion.reshape(2, item_count, FIRST, SECOND)
     spectral = forward_axis(stacked, tables, fresnel_x, row_patterns, False)

time: 308 us -> 347 us (1.13); the launches traced: 308 us -> 341 us
  blocking collectives: 42.1 us -> 96.1 us
  waiting for transfers between devices: 180 us -> 127 us
  local copies, waits for them, and re-layouts: 8.04 us -> 23.1 us
  starting transfers between devices: 34.2 us -> 43.2 us
  other arithmetic: 11.2 us -> 15.2 us
    all_to_all x0 -> x1, blocking collectives: none -> 50.8 us  [column_tail(): lax.all_to_all(stacked_field, 'row', split_axis=1, concat_axis=3, tiled=T...]
    all_gather x1 -> x2, waiting for transfers between devices: 105 us -> 62.8 us  [body(): gathered = lax.all_gather(section_one, 'dir', axis=1, tiled=True)]
    all_to_all x2 -> x3, waiting for transfers between devices: 74.7 us -> 64.1 us  [the longest x2 38 us: column_front(): lax.all_to_all(chunk, 'row', split_axis=0, concat_axis=0, tiled=True)]
    all_to_all x1, blocking collectives: 19.7 us -> 29.9 us  [body(): lax.all_to_all(parts, 'row', split_axis=2, concat_axis=2, tiled=True)]
    all_to_all x2 -> x3, starting transfers between devices: 34 us -> 42.6 us  [the longest x2 27.1 us: column_front(): lax.all_to_all(chunk, 'row', split_axis=0, concat_axis=0, tiled=True)]
    all_to_all x1, blocking collectives: 22.4 us -> 15.3 us  [body(): lax.all_to_all(parts, 'dir', split_axis=1, concat_axis=1, tiled=True)]
    unnamed x13 -> x25, local copies, waits for them, and re-layouts: 0.55 us -> 6.88 us
    another operation x2 -> x7, local copies, waits for them, and re-layouts: 0.27 us -> 5.62 us  [the longest x2 3.16 us: body(): stacked = portion.reshape(2, item_count, FIRST, SECOND)]
  transfers between devices with their start and end apart: 3 -> 5, of which waited for: 3 -> 5; matrix products, arithmetic and copies ran while one was open for 1% -> 6% of each run, Pallas kernels for 0% -> 0%
where the time goes in v3:
time: 347 us; the launch traced here: 341 us
  waiting for transfers between devices  127 us (37%)
  blocking collectives  96.1 us (28%)
  starting transfers between devices  43.2 us (12%)
  local copies, waits for them, and re-layouts  23.1 us (7%)
  matrix products  18.6 us (5%)
  between operations  17.7 us (5%)
  other arithmetic  15.2 us (4%)
    all_gather x2, waiting for transfers between devices, body(): gathered = lax.all_gather(section_one, 'dir', axis=1, tiled=True)  62.8 us
    all_to_all x1, blocking collectives, column_tail(): lax.all_to_all(stacked_field, 'row', split_axis=1, concat_axis=3, tiled=T...  50.8 us
    all_to_all x2, waiting for transfers between devices, column_front(): lax.all_to_all(chunk, 'row', split_axis=0, concat_axis=0, tiled=True)  38 us
    all_to_all x1, blocking collectives, body(): lax.all_to_all(parts, 'row', split_axis=2, concat_axis=2, tiled=True)  29.9 us
    all_to_all x2, starting transfers between devices, column_front(): lax.all_to_all(chunk, 'row', split_axis=0, concat_axis=0, tiled=True)  27.1 us
    all_to_all x1, waiting for transfers between devices, column_tail(): lax.all_to_all(stacked_field, 'row', split_axis=1, concat_axis=3, tiled=T...  26.2 us
    dot_general x18, matrix products, contract(): jnp.einsum(pattern, operand, matrix, preferred_element_type=jnp.float32)  16.1 us
    all_to_all x1, starting transfers between devices, column_tail(): lax.all_to_all(stacked_field, 'row', split_axis=1, concat_axis=3, tiled=T...  15.5 us
  transfers between devices with their start and end apart: 5, of which 5 were waited for; matrix products, arithmetic and copies ran while one was open for 6% of the time, Pallas kernels for 0%

profile of v3, /device:TPU:1, one launch (start us, length us, event | category | flops | bytes accessed | tf_op | source)
XLA Modules:
  0.0 340.9 jit_solution(7422058685448646408)
XLA Ops:
  8.5 1.1 multiply_convert_fusion
  11.3 1.0 reshape.953
  12.3 22.4 %all-to-all-start = ((bf16[64,2,1024]{2,1,0:T(2,128)(2,1)}), bf16[64,2,1024]{2,1,0:T(2,128)(2,1)S(1)}, u32[]{:S(2)}, u32[]{:S(2)}) async-start(bf16[64,2,1024]{2,1,0:T(2,128)(2,1)} %reshape.953), calls=%async_computation | async-start | bytes 524288 | tf_op jit(solution)/shard_map/all_to_all | solution.py:162
  35.2 18.4 %all-to-all-done = bf16[64,2,1024]{2,1,0:T(2,128)(2,1)S(1)} async-done(((bf16[64,2,1024]{2,1,0:T(2,128)(2,1)}), bf16[64,2,1024]{2,1,0:T(2,128)(2,1)S(1)}, u32[]{:S(2)}, u32[]{:S(2)}) %all-to-all-start) | async-done | bytes 262176 | tf_op jit(solution)/shard_map/all_to_all | solution.py:162
  54.4 0.7 pad_maximum_fusion.12
  57.6 1.0 reshape.957
  58.6 4.8 %all-to-all-start.2 = ((bf16[64,2,1024]{2,1,0:T(2,128)(2,1)}), bf16[64,2,1024]{2,1,0:T(2,128)(2,1)S(1)}, u32[]{:S(2)}, u32[]{:S(2)}) async-start(bf16[64,2,1024]{2,1,0:T(2,128)(2,1)} %reshape.957), calls=%async_computation.2 | async-start | bytes 524288 | tf_op jit(solution)/shard_map/all_to_all | solution.py:162
  65.9 19.5 %all-to-all-done.2 = bf16[64,2,1024]{2,1,0:T(2,128)(2,1)S(1)} async-done(((bf16[64,2,1024]{2,1,0:T(2,128)(2,1)}), bf16[64,2,1024]{2,1,0:T(2,128)(2,1)S(1)}, u32[]{:S(2)}, u32[]{:S(2)}) %all-to-all-start.2) | async-done | bytes 262176 | tf_op jit(solution)/shard_map/all_to_all | solution.py:162
  86.1 0.7 pad_maximum_fusion.13
  86.9 39.8 %all-gather.3.cloned.1.call-done = bf16[2,64,128,64]{2,3,1,0:T(8,128)(2,1)} async-done(((bf16[2,8,128,64]{2,3,1,0:T(8,128)(2,1)}), bf16[2,64,128,64]{2,3,1,0:T(8,128)(2,1)}) %all-gather.3.cloned.1.call-update) | async-done | bytes 2097168 | tf_op jit(solution)/shard_map/all_gather | solution.py:218
  126.7 4.1 %cosine_convert_fusion.1 = (bf16[16,128,64]{1,0,2:T(8,128)(2,1)S(1)}, bf16[16,128,64]{1,0,2:T(8,128)(2,1)S(1)}) fusion(f32[]{:T(128)} %bitcast.42, bf16[2,64,128,64]{2,3,1,0:T(8,128)(2,1)} %all-gather.3.cloned.1.call-done, bf16[2,16,64]{2,0,1:T(2,128)(2,1)S(1)} %fusion.157), kind=kOutput, calls=%fused_computation.106 | convolution fusion | flops 33947648 | bytes 2625540 | tf_op jit(solution)/shard_map/zkbx,zak->abx/dot_general | solution.py:98
  132.4 0.7 subtract_convert_fusion.8
  133.4 0.9 convolution_bitcast_fusion.7
  135.5 1.2 copy.442
  138.6 0.7 reshape.955
  139.3 50.8 %all_to_all.53 = bf16[64,2,2048]{2,1,0:T(2,128)(2,1)S(1)} all-to-all(bf16[64,2,2048]{2,1,0:T(2,128)(2,1)S(1)} %reshape.955), channel_id=1, replica_groups=mesh['dir'=8,'row'=64] {'row'}, dimensions={0} | all-to-all | bytes 1048576 | tf_op jit(solution)/shard_map/all_to_all | solution.py:186
  191.6 0.8 all_to_all.40
  192.4 23.0 %all-gather.5.cloned.1.call-done = bf16[2,64,128,64]{2,3,1,0:T(8,128)(2,1)} async-done(((bf16[2,8,128,64]{2,3,1,0:T(8,128)(2,1)}), bf16[2,64,128,64]{2,3,1,0:T(8,128)(2,1)}) %all-gather.5.cloned.1.call-update) | async-done | bytes 2097168 | tf_op jit(solution)/shard_map/all_gather | solution.py:218
  215.4 4.1 %cosine_convert_fusion = (bf16[16,128,64]{1,0,2:T(8,128)(2,1)S(1)}, bf16[16,128,64]{1,0,2:T(8,128)(2,1)S(1)}) fusion(f32[]{:T(128)} %bitcast.42, bf16[2,64,128,64]{2,3,1,0:T(8,128)(2,1)} %all-gather.5.cloned.1.call-done, bf16[2,16,64]{2,0,1:T(2,128)(2,1)S(1)} %fusion.157), kind=kOutput, calls=%fused_computation.104 | convolution fusion | flops 33947648 | bytes 2625540 | tf_op jit(solution)/shard_map/zkbx,zak->abx/dot_general | solution.py:98
  222.1 0.9 convolution_bitcast_fusion.4
  224.2 1.2 copy.441
  227.3 1.6 reshape.959
  228.9 15.5 %all-to-all-start.3 = ((bf16[64,2,2048]{2,1,0:T(2,128)(2,1)}), bf16[64,2,2048]{2,1,0:T(2,128)(2,1)S(1)}, u32[]{:S(2)}, u32[]{:S(2)}) async-start(bf16[64,2,2048]{2,1,0:T(2,128)(2,1)} %reshape.959), calls=%async_computation.3 | async-start | bytes 1048576 | tf_op jit(solution)/shard_map/all_to_all | solution.py:186
  245.9 1.1 stack_reshape.6
  247.1 26.2 %all-to-all-done.3 = bf16[64,2,2048]{2,1,0:T(2,128)(2,1)S(1)} async-done(((bf16[64,2,2048]{2,1,0:T(2,128)(2,1)}), bf16[64,2,2048]{2,1,0:T(2,128)(2,1)S(1)}, u32[]{:S(2)}, u32[]{:S(2)}) %all-to-all-start.3) | async-done | bytes 524320 | tf_op jit(solution)/shard_map/all_to_all | solution.py:186
  275.1 2.2 copy.346
  277.3 1.0 reshape.816
  281.6 1.1 fusion.186
  283.2 2.2 fusion.7
  286.4 29.9 %all_to_all.54 = f32[64,1,256]{2,1,0:T(1,128)S(1)} all-to-all(f32[64,1,256]{2,1,0:T(1,128)S(1)} %reshape.961), channel_id=1, replica_groups=mesh['dir'=8,'row'=64] {'row'}, dimensions={0} | all-to-all | bytes 131072 | tf_op jit(solution)/shard_map/all_to_all | solution.py:260
  316.8 0.8 reduce
  317.9 15.3 %all_to_all.55 = f32[2,8,1,16]{3,0,2,1:T(2,128)S(1)} all-to-all(f32[2,8,1,16]{3,0,2,1:T(2,128)S(1)} %copy.305), channel_id=1, replica_groups=mesh['dir'=8,'row'=64] {'dir'}, dimensions={1} | all-to-all | bytes 2048 | tf_op jit(solution)/shard_map/all_to_all | solution.py:262
  (119 shorter events, 28.1 us)
Async XLA Ops:
  12.3 42.9 %copy-start.5 = (s32[1,2]{1,0:T(1,128)S(1)}, s32[1,2]{1,0:T(1,128)}, u32[]{:S(2)}) copy-start(s32[1,2]{1,0:T(1,128)} %param.9) | copy-start | bytes 28
  12.3 41.4 %all-to-all-start = ((bf16[64,2,1024]{2,1,0:T(2,128)(2,1)}), bf16[64,2,1024]{2,1,0:T(2,128)(2,1)S(1)}, u32[]{:S(2)}, u32[]{:S(2)}) async-start(bf16[64,2,1024]{2,1,0:T(2,128)(2,1)} %reshape.953), calls=%async_computation | async-start | bytes 524288 | tf_op jit(solution)/shard_map/all_to_all | solution.py:162
  34.7 92.1 %all-gather.3.cloned.1.call-start = ((), (), s32[]{:S(2)}) async-start(), calls=%async_computation.6 | async-start | bytes 2359296 | tf_op jit(solution)/shard_map/all_gather | solution.py:218
  58.6 26.8 %all-to-all-start.2 = ((bf16[64,2,1024]{2,1,0:T(2,128)(2,1)}), bf16[64,2,1024]{2,1,0:T(2,128)(2,1)S(1)}, u32[]{:S(2)}, u32[]{:S(2)}) async-start(bf16[64,2,1024]{2,1,0:T(2,128)(2,1)} %reshape.957), calls=%async_computation.2 | async-start | bytes 524288 | tf_op jit(solution)/shard_map/all_to_all | solution.py:162
  63.4 152.1 %all-gather.5.cloned.1.call-start = ((), (), s32[]{:S(2)}) async-start(), calls=%async_computation.7 | async-start | bytes 2359296 | tf_op jit(solution)/shard_map/all_gather | solution.py:218
  226.6 18.6 %copy-start.3 = (s32[1,8192]{1,0:T(1,128)S(1)}, s32[1,8192]{1,0:T(1,128)}, u32[]{:S(2)}) copy-start(s32[1,8192]{1,0:T(1,128)} %param.11) | copy-start | bytes 98308
  228.9 44.4 %all-to-all-start.3 = ((bf16[64,2,2048]{2,1,0:T(2,128)(2,1)}), bf16[64,2,2048]{2,1,0:T(2,128)(2,1)S(1)}, u32[]{:S(2)}, u32[]{:S(2)}) async-start(bf16[64,2,2048]{2,1,0:T(2,128)(2,1)} %reshape.959), calls=%async_computation.3 | async-start | bytes 1048576 | tf_op jit(solution)/shard_map/all_to_all | solution.py:186
  281.6 1.6 copy-start.1
  281.6 1.6 copy-start.2
  283.0 2.5 copy-start
  283.0 2.5 copy-start.4
  283.2 2.3 copy-start.6
Sparse Core Ops, SparseCore 0:
  55.3 71.3 all-gather.2
  128.8 86.5 all-gather.4

commit v4 on v2

--- a/solution.py
+++ b/solution.py
@@ -190,20 +190,19 @@
     section_one = complex_times(
         contract("khzrx,wzbhr->wkbx", stacked, inner_split), twist_real, -twist_imag
     )
-    section_one = section_one.astype(jnp.bfloat16)
+    section_one = jnp.transpose(section_one.astype(jnp.bfloat16), (1, 0, 2, 3))
     outer_count = patch_len // SECOND
     outer_ids = (offset_rows // SECOND + jnp.arange(outer_count, dtype=jnp.int32)) % FIRST
     patch_outer = jnp.take(tables[0][0], outer_ids, axis=1)
     phase_patch = contract(
-        "zkbx,zak->abx", lax.all_gather(section_one, "dir", axis=1, tiled=True), patch_outer
+        "kzbx,zak->abx", lax.all_gather(section_one, "dir", axis=0, tiled=True), patch_outer
     )
     phase_patch = phase_patch.reshape(patch_len, columns) * (1.0 / N)
     screen_field = propagate_columns(phase_patch, tables_y, slant_factor, fresnel_y)
-    stacked_field = screen_field.reshape(2, row_count, ROWS_DEV, columns)
-    portion = lax.all_to_all(stacked_field, "row", split_axis=1, concat_axis=3, tiled=True)
+    stacked_field = jnp.transpose(screen_field.reshape(2, row_count, ROWS_DEV, columns), (1, 0, 2, 3))
+    portion = lax.all_to_all(stacked_field, "row", split_axis=0, concat_axis=0, tiled=True)
     item_count = portion.shape[2]
-    stacked = portion.reshape(2, item_count, FIRST, SECOND)
-    spectral = forward_axis(stacked, tables, fresnel_x, row_patterns, False)
+    spectral = forward_axis(portion, tables, fresnel_x, ("azrb,zwak->wrkb",) + row_patterns[1:], False)
     wave_field = inverse_axis(spectral, tables, row_patterns, False)
     intensity = wave_field[0] * wave_field[0] + wave_field[1] * wave_field[1]
     intensity = intensity.reshape(item_count, XTILES, TILE_X)

time: 308 us -> 309 us (level)
  no operation moved by 1% of the time
where the time goes in v4:
time: 309 us
  waiting for transfers between devices  180 us (58%)
  blocking collectives  42.1 us (14%)
  starting transfers between devices  34.2 us (11%)
  between operations  17.2 us (6%)
  matrix products  15.7 us (5%)
  other arithmetic  11.2 us (4%)
  local copies, waits for them, and re-layouts  8.44 us (3%)
    all_gather x1, waiting for transfers between devices, body(): lax.all_gather(section_one, 'dir', axis=0, tiled=True)  105 us
    all_to_all x1, waiting for transfers between devices, body(): lax.all_to_all(stacked_field, 'row', split_axis=0, concat_axis=0, tiled=T...  53.6 us
    all_to_all x1, blocking collectives, body(): lax.all_to_all(parts, 'dir', split_axis=1, concat_axis=1, tiled=True)  22.5 us
    all_to_all x1, starting transfers between devices, body(): lax.all_to_all(half_screen, 'row', split_axis=0, concat_axis=0, tiled=True)  22.2 us
    all_to_all x1, waiting for transfers between devices, body(): lax.all_to_all(half_screen, 'row', split_axis=0, concat_axis=0, tiled=True)  21.1 us
    all_to_all x1, blocking collectives, body(): lax.all_to_all(parts, 'row', split_axis=2, concat_axis=2, tiled=True)  19.7 us
    dot_general x12, matrix products, contract(): jnp.einsum(pattern, operand, matrix, preferred_element_type=jnp.float32)  13.1 us
    all_to_all x1, starting transfers between devices, body(): lax.all_to_all(stacked_field, 'row', split_axis=0, concat_axis=0, tiled=T...  11.7 us
  transfers between devices with their start and end apart: 3, of which 3 were waited for; matrix products, arithmetic and copies ran while one was open for 1% of the time, Pallas kernels for 0%

profile of v4, /device:TPU:1, one launch (start us, length us, event | category | flops | bytes accessed | tf_op | source)
XLA Modules:
  0.0 308.8 jit_solution(16566696142698562467)
XLA Ops:
  8.5 1.1 multiply_convert_fusion
  10.7 1.1 copy.139
  11.8 22.2 %all-to-all-start = ((bf16[64,2,16,128]{3,2,1,0:T(8,128)(2,1)}), bf16[64,2,16,128]{3,2,1,0:T(8,128)(2,1)S(1)}, u32[]{:S(2)}, u32[]{:S(2)}) async-start(bf16[64,2,16,128]{3,2,1,0:T(8,128)(2,1)} %copy.139), calls=%async_computation | async-start | bytes 1048576 | tf_op jit(solution)/shard_map/all_to_all | solution.py:177
  34.5 0.3 negate_convert_fusion
  34.8 21.1 %all-to-all-done = bf16[64,2,16,128]{3,2,1,0:T(8,128)(2,1)S(1)} async-done(((bf16[64,2,16,128]{3,2,1,0:T(8,128)(2,1)}), bf16[64,2,16,128]{3,2,1,0:T(8,128)(2,1)S(1)}, u32[]{:S(2)}, u32[]{:S(2)}) %all-to-all-start) | async-done | bytes 524320 | tf_op jit(solution)/shard_map/all_to_all | solution.py:177
  56.6 0.8 maximum_bitcast_fusion.3
  57.5 0.6 fusion.173
  60.4 0.6 gather_fusion
  61.5 105.2 %all-gather.2.cloned.1.call-done = bf16[64,2,128,128]{3,2,0,1:T(8,128)(2,1)} async-done(((bf16[8,2,128,128]{3,2,0,1:T(8,128)(2,1)}), bf16[64,2,128,128]{3,2,0,1:T(8,128)(2,1)}) %all-gather.2.cloned.1.call-update) | async-done | bytes 4194320 | tf_op jit(solution)/shard_map/all_gather | solution.py:198
  166.7 7.0 %cosine_convert_fusion = (bf16[16,128,128]{2,0,1:T(8,128)(2,1)S(1)}, bf16[16,128,128]{2,0,1:T(8,128)(2,1)S(1)}) fusion(f32[]{:T(128)} %bitcast.44, bf16[64,2,128,128]{3,2,0,1:T(8,128)(2,1)} %all-gather.2.cloned.1.call-done, bf16[2,16,64]{2,0,1:T(2,128)(2,1)S(1)} %fusion.144), kind=kOutput, calls=%fused_computation.68 | convolution fusion | flops 67895296 | bytes 5246980 | tf_op jit(solution)/shard_map/kzbx,zak->abx/dot_general | solution.py:98
  174.5 0.5 convolution_bitcast_fusion.5
  174.9 0.7 subtract_convert_fusion.5
  175.7 0.9 convolution_bitcast_fusion.4
  176.6 0.7 subtract_convert_fusion.4
  177.3 0.5 convolution_bitcast_fusion.3
  177.8 1.2 copy.257
  179.0 0.7 subtract_convert_fusion.3
  179.7 0.5 fusion.6
  180.2 2.1 copy.154
  182.3 11.7 %all-to-all-start.1 = ((bf16[64,2,32,128]{3,1,2,0:T(2,128)(2,1)}), bf16[64,2,32,128]{3,1,2,0:T(2,128)(2,1)S(1)}, u32[]{:S(2)}, u32[]{:S(2)}) async-start(bf16[64,2,32,128]{3,1,2,0:T(2,128)(2,1)} %copy.154), calls=%async_computation.1 | async-start | bytes 2097152 | tf_op jit(solution)/shard_map/all_to_all | solution.py:203
  194.9 53.6 %all-to-all-done.1 = bf16[64,2,32,128]{3,1,2,0:T(2,128)(2,1)S(1)} async-done(((bf16[64,2,32,128]{3,1,2,0:T(2,128)(2,1)}), bf16[64,2,32,128]{3,1,2,0:T(2,128)(2,1)S(1)}, u32[]{:S(2)}, u32[]{:S(2)}) %all-to-all-start.1) | async-done | bytes 1048608 | tf_op jit(solution)/shard_map/all_to_all | solution.py:203
  248.5 1.4 convolution_bitcast_fusion.2
  250.3 0.4 convolution_bitcast_fusion.1
  251.0 0.5 convolution_bitcast_fusion
  251.8 0.5 fusion.2
  252.9 1.1 fusion.172
  254.4 2.3 fusion.4
  257.6 19.7 %all_to_all.20 = f32[64,1,256]{2,1,0:T(1,128)S(1)} all-to-all(f32[64,1,256]{2,1,0:T(1,128)S(1)} %reshape.945), channel_id=1, replica_groups=mesh['dir'=8,'row'=64] {'row'}, dimensions={0} | all-to-all | bytes 131072 | tf_op jit(solution)/shard_map/all_to_all | solution.py:233
  277.3 0.5 broadcast.1446
  277.8 0.8 reduce
  278.9 22.5 %all_to_all.21 = f32[2,8,1,16]{3,0,2,1:T(2,128)S(1)} all-to-all(f32[2,8,1,16]{3,0,2,1:T(2,128)S(1)} %copy.164), channel_id=1, replica_groups=mesh['dir'=8,'row'=64] {'dir'}, dimensions={1} | all-to-all | bytes 2048 | tf_op jit(solution)/shard_map/all_to_all | solution.py:235
  301.4 0.5 multiply_bitcast_fusion
  (73 shorter events, 8.2 us)
Async XLA Ops:
  11.8 44.1 %all-to-all-start = ((bf16[64,2,16,128]{3,2,1,0:T(8,128)(2,1)}), bf16[64,2,16,128]{3,2,1,0:T(8,128)(2,1)S(1)}, u32[]{:S(2)}, u32[]{:S(2)}) async-start(bf16[64,2,16,128]{3,2,1,0:T(8,128)(2,1)} %copy.139), calls=%async_computation | async-start | bytes 1048576 | tf_op jit(solution)/shard_map/all_to_all | solution.py:177
  34.1 132.6 %all-gather.2.cloned.1.call-start = ((), (), s32[]{:S(2)}) async-start(), calls=%async_computation.4 | async-start | bytes 4718592 | tf_op jit(solution)/shard_map/all_gather | solution.py:198
  55.9 1.5 copy-start.3
  180.2 14.6 %copy-start.1 = (s32[1,8192]{1,0:T(1,128)S(1)}, s32[1,8192]{1,0:T(1,128)}, u32[]{:S(2)}) copy-start(s32[1,8192]{1,0:T(1,128)} %param.9) | copy-start | bytes 98308
  182.3 66.2 %all-to-all-start.1 = ((bf16[64,2,32,128]{3,1,2,0:T(2,128)(2,1)}), bf16[64,2,32,128]{3,1,2,0:T(2,128)(2,1)S(1)}, u32[]{:S(2)}, u32[]{:S(2)}) async-start(bf16[64,2,32,128]{3,1,2,0:T(2,128)(2,1)} %copy.154), calls=%async_computation.1 | async-start | bytes 2097152 | tf_op jit(solution)/shard_map/all_to_all | solution.py:203
  254.2 2.5 copy-start
  254.2 2.5 copy-start.2
  254.4 2.3 copy-start.4
Sparse Core Ops, SparseCore 0:
  57.6 109.0 all-gather.1

commit v5 on v2

--- a/solution.py
+++ b/solution.py
@@ -194,8 +194,11 @@
     outer_count = patch_len // SECOND
     outer_ids = (offset_rows // SECOND + jnp.arange(outer_count, dtype=jnp.int32)) % FIRST
     patch_outer = jnp.take(tables[0][0], outer_ids, axis=1)
-    phase_patch = contract(
-        "zkbx,zak->abx", lax.all_gather(section_one, "dir", axis=1, tiled=True), patch_outer
+    gathered = lax.all_gather(section_one, "dir", axis=1, tiled=True)
+    depth = gathered.shape[0] * gathered.shape[1]
+    patch_matrix = jnp.transpose(patch_outer, (1, 0, 2)).reshape(outer_count, depth)
+    phase_patch = jnp.dot(
+        patch_matrix, gathered.reshape(depth, -1), preferred_element_type=jnp.float32
     )
     phase_patch = phase_patch.reshape(patch_len, columns) * (1.0 / N)
     screen_field = propagate_columns(phase_patch, tables_y, slant_factor, fresnel_y)

time: 308 us -> 308 us (level)
    dot_general x12 -> x11, matrix products: 12.6 us -> 5.52 us  [contract(): jnp.einsum(pattern, operand, matrix, preferred_element_type=jnp.float32)]
    dot_general x0 -> x1, matrix products: none -> 6.98 us  [body(): jnp.dot(patch_matrix, gathered.reshape(depth, -1), preferred_element_type...]
where the time goes in v5:
time: 308 us
  waiting for transfers between devices  180 us (58%)
  blocking collectives  42.1 us (14%)
  starting transfers between devices  34.2 us (11%)
  between operations  17.2 us (6%)
  matrix products  15.1 us (5%)
  other arithmetic  11.2 us (4%)
  local copies, waits for them, and re-layouts  8.34 us (3%)
    all_gather x1, waiting for transfers between devices, body(): gathered = lax.all_gather(section_one, 'dir', axis=1, tiled=True)  105 us
    all_to_all x1, waiting for transfers between devices, body(): lax.all_to_all(stacked_field, 'row', split_axis=1, concat_axis=3, tiled=T...  53.6 us
    all_to_all x1, blocking collectives, body(): lax.all_to_all(parts, 'dir', split_axis=1, concat_axis=1, tiled=True)  22.5 us
    all_to_all x1, starting transfers between devices, body(): lax.all_to_all(half_screen, 'row', split_axis=0, concat_axis=0, tiled=True)  22.2 us
    all_to_all x1, waiting for transfers between devices, body(): lax.all_to_all(half_screen, 'row', split_axis=0, concat_axis=0, tiled=True)  21.1 us
    all_to_all x1, blocking collectives, body(): lax.all_to_all(parts, 'row', split_axis=2, concat_axis=2, tiled=True)  19.7 us
    all_to_all x1, starting transfers between devices, body(): lax.all_to_all(stacked_field, 'row', split_axis=1, concat_axis=3, tiled=T...  11.7 us
    dot_general x1, matrix products, body(): jnp.dot(patch_matrix, gathered.reshape(depth, -1), preferred_element_type...  6.98 us
  transfers between devices with their start and end apart: 3, of which 3 were waited for; matrix products, arithmetic and copies ran while one was open for 1% of the time, Pallas kernels for 0%

profile of v5, /device:TPU:1, one launch (start us, length us, event | category | flops | bytes accessed | tf_op | source)
XLA Modules:
  0.0 308.0 jit_solution(7845668537550532595)
XLA Ops:
  8.5 1.1 multiply_convert_fusion
  10.7 1.1 copy.128
  11.8 22.2 %all-to-all-start = ((bf16[64,2,16,128]{3,2,1,0:T(8,128)(2,1)}), bf16[64,2,16,128]{3,2,1,0:T(8,128)(2,1)S(1)}, u32[]{:S(2)}, u32[]{:S(2)}) async-start(bf16[64,2,16,128]{3,2,1,0:T(8,128)(2,1)} %copy.128), calls=%async_computation | async-start | bytes 1048576 | tf_op jit(solution)/shard_map/all_to_all | solution.py:177
  34.5 0.3 negate_convert_fusion
  34.8 21.1 %all-to-all-done = bf16[64,2,16,128]{3,2,1,0:T(8,128)(2,1)S(1)} async-done(((bf16[64,2,16,128]{3,2,1,0:T(8,128)(2,1)}), bf16[64,2,16,128]{3,2,1,0:T(8,128)(2,1)S(1)}, u32[]{:S(2)}, u32[]{:S(2)}) %all-to-all-start) | async-done | bytes 524320 | tf_op jit(solution)/shard_map/all_to_all | solution.py:177
  56.6 0.8 pad_maximum_fusion.7
  57.5 0.6 fusion.162
  59.4 0.6 gather_fusion
  61.6 105.1 %all-gather.2.cloned.1.call-done = bf16[2,64,128,128]{3,2,1,0:T(8,128)(2,1)} async-done(((bf16[2,8,128,128]{3,2,1,0:T(8,128)(2,1)}), bf16[2,64,128,128]{3,2,1,0:T(8,128)(2,1)}) %all-gather.2.cloned.1.call-update) | async-done | bytes 4194320 | tf_op jit(solution)/shard_map/all_gather | solution.py:197
  166.7 7.0 %cosine_convert_fusion = (bf16[16,16384]{1,0:T(8,128)(2,1)S(1)}, bf16[16,16384]{1,0:T(8,128)(2,1)S(1)}) fusion(f32[]{:T(128)} %bitcast.39, bf16[16,128]{1,0:T(8,128)(2,1)S(1)} %reshape.779, bf16[16,8,128,128]{3,2,1,0:T(8,128)(2,1)} %bitcast.203), kind=kOutput, calls=%fused_computation.67 | convolution fusion | flops 67895296 | bytes 5246980 | tf_op jit(solution)/shard_map/dot_general | solution.py:200
  174.6 0.5 convolution_bitcast_fusion.5
  175.1 0.7 subtract_convert_fusion.5
  175.9 0.9 convolution_bitcast_fusion.4
  176.8 0.7 subtract_convert_fusion.4
  177.5 0.5 convolution_bitcast_fusion.3
  177.9 1.2 copy.233
  179.2 0.7 subtract_convert_fusion.3
  179.9 0.5 fusion.3
  180.4 1.7 copy.139
  182.0 11.7 %all-to-all-start.1 = ((bf16[2,64,32,128]{3,2,0,1:T(8,128)(2,1)}), bf16[2,64,32,128]{3,2,0,1:T(8,128)(2,1)S(1)}, u32[]{:S(2)}, u32[]{:S(2)}) async-start(bf16[2,64,32,128]{3,2,0,1:T(8,128)(2,1)} %copy.139), calls=%async_computation.1 | async-start | bytes 2097152 | tf_op jit(solution)/shard_map/all_to_all | solution.py:206
  194.7 53.6 %all-to-all-done.1 = bf16[2,64,32,128]{3,2,0,1:T(8,128)(2,1)S(1)} async-done(((bf16[2,64,32,128]{3,2,0,1:T(8,128)(2,1)}), bf16[2,64,32,128]{3,2,0,1:T(8,128)(2,1)S(1)}, u32[]{:S(2)}, u32[]{:S(2)}) %all-to-all-start.1) | async-done | bytes 1048608 | tf_op jit(solution)/shard_map/all_to_all | solution.py:206
  248.3 0.9 convolution_bitcast_fusion.2
  249.5 0.4 convolution_bitcast_fusion.1
  250.2 0.5 convolution_bitcast_fusion
  251.0 0.5 fusion.2
  252.1 1.1 fusion.161
  253.6 2.3 fusion.4
  256.8 19.7 %all_to_all.30 = f32[64,1,256]{2,1,0:T(1,128)S(1)} all-to-all(f32[64,1,256]{2,1,0:T(1,128)S(1)} %reshape.956), channel_id=1, replica_groups=mesh['dir'=8,'row'=64] {'row'}, dimensions={0} | all-to-all | bytes 131072 | tf_op jit(solution)/shard_map/all_to_all | solution.py:237
  276.5 0.5 broadcast.1446
  277.0 0.8 reduce
  278.1 22.5 %all_to_all.31 = f32[2,8,1,16]{3,0,2,1:T(2,128)S(1)} all-to-all(f32[2,8,1,16]{3,0,2,1:T(2,128)S(1)} %copy.149), channel_id=1, replica_groups=mesh['dir'=8,'row'=64] {'dir'}, dimensions={1} | all-to-all | bytes 2048 | tf_op jit(solution)/shard_map/all_to_all | solution.py:239
  300.6 0.5 multiply_bitcast_fusion
  (74 shorter events, 8.5 us)
Async XLA Ops:
  11.8 44.1 %all-to-all-start = ((bf16[64,2,16,128]{3,2,1,0:T(8,128)(2,1)}), bf16[64,2,16,128]{3,2,1,0:T(8,128)(2,1)S(1)}, u32[]{:S(2)}, u32[]{:S(2)}) async-start(bf16[64,2,16,128]{3,2,1,0:T(8,128)(2,1)} %copy.128), calls=%async_computation | async-start | bytes 1048576 | tf_op jit(solution)/shard_map/all_to_all | solution.py:177
  34.1 132.6 %all-gather.2.cloned.1.call-start = ((), (), s32[]{:S(2)}) async-start(), calls=%async_computation.4 | async-start | bytes 4718592 | tf_op jit(solution)/shard_map/all_gather | solution.py:197
  55.9 1.5 copy-start.3
  180.4 14.2 %copy-start.1 = (s32[1,8192]{1,0:T(1,128)S(1)}, s32[1,8192]{1,0:T(1,128)}, u32[]{:S(2)}) copy-start(s32[1,8192]{1,0:T(1,128)} %param.9) | copy-start | bytes 98308
  182.0 66.2 %all-to-all-start.1 = ((bf16[2,64,32,128]{3,2,0,1:T(8,128)(2,1)}), bf16[2,64,32,128]{3,2,0,1:T(8,128)(2,1)S(1)}, u32[]{:S(2)}, u32[]{:S(2)}) async-start(bf16[2,64,32,128]{3,2,0,1:T(8,128)(2,1)} %copy.139), calls=%async_computation.1 | async-start | bytes 2097152 | tf_op jit(solution)/shard_map/all_to_all | solution.py:206
  253.4 2.5 copy-start
  253.4 2.5 copy-start.2
  253.6 2.3 copy-start.4
Sparse Core Ops, SparseCore 0:
  57.6 109.0 all-gather.1

commit v6 on v5

--- a/solution.py
+++ b/solution.py
@@ -145,13 +145,34 @@
     return (fluctuation, mean_one * jnp.exp(-fluctuation))
 
 
+def turn_pair(angle):
+    quarter = jnp.round(angle * (2.0 / 3.141592653589793))
+    rest = angle - quarter * 1.5703125
+    rest = rest - quarter * 4.837512969970703125e-4
+    rest = rest - quarter * 7.54978995489188216e-8
+    square = rest * rest
+    sine = rest + rest * square * (
+        -1.6666654611e-1 + square * (8.3321608736e-3 + square * -1.9515295891e-4)
+    )
+    cosine = 1.0 - 0.5 * square + square * square * (
+        4.166664568298827e-2 + square * (-1.388731625493765e-3 + square * 2.443315711809948e-5)
+    )
+    turn = quarter.astype(jnp.int32) & 3
+    swap = (turn & 1) == 1
+    sin_value = jnp.where(swap, cosine, sine)
+    cos_value = jnp.where(swap, sine, cosine)
+    sin_value = jnp.where(turn >= 2, -sin_value, sin_value)
+    cos_value = jnp.where((turn == 1) | (turn == 2), -cos_value, cos_value)
+    return cos_value, sin_value
+
+
 def propagate_columns(phase_patch, tables_y, slant_factor, fresnel_y):
     patch_rows = phase_patch.shape[0]
     width_here = phase_patch.shape[1]
     outer_len = tables_y[0].shape[2]
     inner_len = tables_y[1].shape[2]
     turned_phase = slant_factor * phase_patch
-    screen_field = jnp.stack([jnp.cos(turned_phase), jnp.sin(turned_phase)]).astype(jnp.bfloat16)
+    screen_field = jnp.stack(turn_pair(turned_phase)).astype(jnp.bfloat16)
     stacked = screen_field.reshape(2, outer_len, inner_len, width_here)
     spectral = forward_axis(stacked, tables_y, fresnel_y, column_patterns, True)
     result = inverse_axis(spectral, tables_y, column_patterns, True)

time: 308 us -> 307 us (level)
    another operation x15 -> x16, other arithmetic: 4.9 us -> 6.5 us
where the time goes in v6:
time: 307 us; the launch traced here: 306 us
  waiting for transfers between devices  180 us (59%)
  blocking collectives  42.1 us (14%)
  starting transfers between devices  34.2 us (11%)
  between operations  17.2 us (6%)
  other arithmetic  12.8 us (4%)
  matrix products  12.6 us (4%)
  local copies, waits for them, and re-layouts  7.6 us (2%)
    all_gather x1, waiting for transfers between devices, body(): gathered = lax.all_gather(section_one, 'dir', axis=1, tiled=True)  105 us
    all_to_all x1, waiting for transfers between devices, body(): lax.all_to_all(stacked_field, 'row', split_axis=1, concat_axis=3, tiled=T...  53.6 us
    all_to_all x1, blocking collectives, body(): lax.all_to_all(parts, 'dir', split_axis=1, concat_axis=1, tiled=True)  22.5 us
    all_to_all x1, starting transfers between devices, body(): lax.all_to_all(half_screen, 'row', split_axis=0, concat_axis=0, tiled=True)  22.2 us
    all_to_all x1, waiting for transfers between devices, body(): lax.all_to_all(half_screen, 'row', split_axis=0, concat_axis=0, tiled=True)  21.1 us
    all_to_all x1, blocking collectives, body(): lax.all_to_all(parts, 'row', split_axis=2, concat_axis=2, tiled=True)  19.7 us
    all_to_all x1, starting transfers between devices, body(): lax.all_to_all(stacked_field, 'row', split_axis=1, concat_axis=3, tiled=T...  11.7 us
    another operation x16, other arithmetic  6.5 us
  transfers between devices with their start and end apart: 3, of which 3 were waited for; matrix products, arithmetic and copies ran while one was open for 1% of the time, Pallas kernels for 0%

profile of v6, /device:TPU:1, one launch (start us, length us, event | category | flops | bytes accessed | tf_op | source)
XLA Modules:
  0.0 306.3 jit_solution(62604927626251971)
XLA Ops:
  8.5 1.1 multiply_convert_fusion
  10.7 1.1 copy.128
  11.8 22.2 %all-to-all-start = ((bf16[64,2,16,128]{3,2,1,0:T(8,128)(2,1)}), bf16[64,2,16,128]{3,2,1,0:T(8,128)(2,1)S(1)}, u32[]{:S(2)}, u32[]{:S(2)}) async-start(bf16[64,2,16,128]{3,2,1,0:T(8,128)(2,1)} %copy.128), calls=%async_computation | async-start | bytes 1048576 | tf_op jit(solution)/shard_map/all_to_all | solution.py:198
  34.8 21.1 %all-to-all-done = bf16[64,2,16,128]{3,2,1,0:T(8,128)(2,1)S(1)} async-done(((bf16[64,2,16,128]{3,2,1,0:T(8,128)(2,1)}), bf16[64,2,16,128]{3,2,1,0:T(8,128)(2,1)S(1)}, u32[]{:S(2)}, u32[]{:S(2)}) %all-to-all-start) | async-done | bytes 524320 | tf_op jit(solution)/shard_map/all_to_all | solution.py:198
  56.6 0.8 pad_maximum_fusion.7
  57.5 0.6 fusion.173
  59.4 0.6 gather_fusion
  61.6 105.1 %all-gather.2.cloned.1.call-done = bf16[2,64,128,128]{3,2,1,0:T(8,128)(2,1)} async-done(((bf16[2,8,128,128]{3,2,1,0:T(8,128)(2,1)}), bf16[2,64,128,128]{3,2,1,0:T(8,128)(2,1)}) %all-gather.2.cloned.1.call-update) | async-done | bytes 4194320 | tf_op jit(solution)/shard_map/all_gather | solution.py:218
  166.7 4.5 %convolution_multiply_fusion = f32[16,16384]{1,0:T(8,128)S(1)} fusion(bf16[16,128]{1,0:T(8,128)(2,1)S(1)} %reshape.886, bf16[16,8,128,128]{3,2,1,0:T(8,128)(2,1)} %bitcast.201, f32[]{:T(128)} %bitcast.39), kind=kOutput, calls=%fused_computation.1 | convolution fusion | flops 67371008 | bytes 5246980 | tf_op jit(solution)/shard_map/dot_general | solution.py:221
  171.4 1.6 fusion.18
  173.0 0.5 convolution_bitcast_fusion.5
  173.4 0.7 subtract_convert_fusion.5
  174.3 0.9 convolution_bitcast_fusion.4
  175.2 0.7 subtract_convert_fusion.4
  175.9 0.5 convolution_bitcast_fusion.3
  176.3 1.2 copy.255
  177.5 0.7 subtract_convert_fusion.3
  178.3 0.5 fusion.3
  178.8 1.7 copy.139
  180.4 11.7 %all-to-all-start.1 = ((bf16[2,64,32,128]{3,2,0,1:T(8,128)(2,1)}), bf16[2,64,32,128]{3,2,0,1:T(8,128)(2,1)S(1)}, u32[]{:S(2)}, u32[]{:S(2)}) async-start(bf16[2,64,32,128]{3,2,0,1:T(8,128)(2,1)} %copy.139), calls=%async_computation.1 | async-start | bytes 2097152 | tf_op jit(solution)/shard_map/all_to_all | solution.py:227
  193.1 53.6 %all-to-all-done.1 = bf16[2,64,32,128]{3,2,0,1:T(8,128)(2,1)S(1)} async-done(((bf16[2,64,32,128]{3,2,0,1:T(8,128)(2,1)}), bf16[2,64,32,128]{3,2,0,1:T(8,128)(2,1)S(1)}, u32[]{:S(2)}, u32[]{:S(2)}) %all-to-all-start.1) | async-done | bytes 1048608 | tf_op jit(solution)/shard_map/all_to_all | solution.py:227
  246.6 0.9 convolution_bitcast_fusion.2
  247.8 0.4 convolution_bitcast_fusion.1
  248.6 0.5 convolution_bitcast_fusion
  249.4 0.5 fusion.2
  250.4 1.1 fusion.172
  252.0 2.3 fusion.4
  255.2 19.7 %all_to_all.30 = f32[64,1,256]{2,1,0:T(1,128)S(1)} all-to-all(f32[64,1,256]{2,1,0:T(1,128)S(1)} %reshape.1063), channel_id=1, replica_groups=mesh['dir'=8,'row'=64] {'row'}, dimensions={0} | all-to-all | bytes 131072 | tf_op jit(solution)/shard_map/all_to_all | solution.py:258
  274.9 0.5 broadcast.1677
  275.4 0.8 reduce
  276.5 22.5 %all_to_all.31 = f32[2,8,1,16]{3,0,2,1:T(2,128)S(1)} all-to-all(f32[2,8,1,16]{3,0,2,1:T(2,128)S(1)} %copy.149), channel_id=1, replica_groups=mesh['dir'=8,'row'=64] {'dir'}, dimensions={1} | all-to-all | bytes 2048 | tf_op jit(solution)/shard_map/all_to_all | solution.py:260
  299.0 0.5 multiply_bitcast_fusion
  (72 shorter events, 8.1 us)
Async XLA Ops:
  11.8 44.1 %all-to-all-start = ((bf16[64,2,16,128]{3,2,1,0:T(8,128)(2,1)}), bf16[64,2,16,128]{3,2,1,0:T(8,128)(2,1)S(1)}, u32[]{:S(2)}, u32[]{:S(2)}) async-start(bf16[64,2,16,128]{3,2,1,0:T(8,128)(2,1)} %copy.128), calls=%async_computation | async-start | bytes 1048576 | tf_op jit(solution)/shard_map/all_to_all | solution.py:198
  34.1 132.6 %all-gather.2.cloned.1.call-start = ((), (), s32[]{:S(2)}) async-start(), calls=%async_computation.4 | async-start | bytes 4718592 | tf_op jit(solution)/shard_map/all_gather | solution.py:218
  55.9 1.5 copy-start.3
  178.7 14.2 %copy-start.1 = (s32[1,8192]{1,0:T(1,128)S(1)}, s32[1,8192]{1,0:T(1,128)}, u32[]{:S(2)}) copy-start(s32[1,8192]{1,0:T(1,128)} %param.9) | copy-start | bytes 98308
  180.4 66.2 %all-to-all-start.1 = ((bf16[2,64,32,128]{3,2,0,1:T(8,128)(2,1)}), bf16[2,64,32,128]{3,2,0,1:T(8,128)(2,1)S(1)}, u32[]{:S(2)}, u32[]{:S(2)}) async-start(bf16[2,64,32,128]{3,2,0,1:T(8,128)(2,1)} %copy.139), calls=%async_computation.1 | async-start | bytes 2097152 | tf_op jit(solution)/shard_map/all_to_all | solution.py:227
  251.8 2.5 copy-start
  251.8 2.5 copy-start.2
  252.0 2.3 copy-start.4
Sparse Core Ops, SparseCore 0:
  57.6 109.0 all-gather.1

commit v7 on v6

--- a/solution.py
+++ b/solution.py
@@ -242,8 +242,15 @@
     inside = (local_tile >= 0) & (local_tile < tile_total)
     tile_row = local_tile // XTILES
     tile_column = local_tile % XTILES
-    pick_row = (tile_row[:, None] == jnp.arange(YTILES, dtype=jnp.int32)[None, :]).astype(jnp.float32)
-    row_values = jnp.dot(pick_row, faded_power, precision=lax.Precision.HIGHEST)
+    pick_row = (tile_row[:, None] == jnp.arange(YTILES, dtype=jnp.int32)[None, :]).astype(jnp.bfloat16)
+    high_part = faded_power.astype(jnp.bfloat16)
+    middle_rest = faded_power - high_part.astype(jnp.float32)
+    middle_part = middle_rest.astype(jnp.bfloat16)
+    low_part = (middle_rest - middle_part.astype(jnp.float32)).astype(jnp.bfloat16)
+    split_parts = jnp.concatenate([high_part, middle_part, low_part], axis=1)
+    row_parts = jnp.dot(pick_row, split_parts, preferred_element_type=jnp.float32)
+    row_parts = row_parts.reshape(-1, 3, XTILES)
+    row_values = (row_parts[:, 0] + row_parts[:, 1]) + row_parts[:, 2]
     pick_column = tile_column[:, None] == jnp.arange(XTILES, dtype=jnp.int32)[None, :]
     looked = jnp.sum(jnp.where(pick_column, row_values, 0.0), axis=1)
     looked = jnp.where(inside, looked, 0.0)

time: 307 us -> 308 us (level)
  no operation moved by 1% of the time
where the time goes in v7:
time: 308 us
  waiting for transfers between devices  180 us (58%)
  blocking collectives  42.1 us (14%)
  starting transfers between devices  34.2 us (11%)
  between operations  17.2 us (6%)
  other arithmetic  14 us (5%)
  matrix products  12.8 us (4%)
  local copies, waits for them, and re-layouts  7.6 us (2%)
    all_gather x1, waiting for transfers between devices, body(): gathered = lax.all_gather(section_one, 'dir', axis=1, tiled=True)  105 us
    all_to_all x1, waiting for transfers between devices, body(): lax.all_to_all(stacked_field, 'row', split_axis=1, concat_axis=3, tiled=T...  53.6 us
    all_to_all x1, blocking collectives, body(): lax.all_to_all(parts, 'dir', split_axis=1, concat_axis=1, tiled=True)  22.5 us
    all_to_all x1, starting transfers between devices, body(): lax.all_to_all(half_screen, 'row', split_axis=0, concat_axis=0, tiled=True)  22.2 us
    all_to_all x1, waiting for transfers between devices, body(): lax.all_to_all(half_screen, 'row', split_axis=0, concat_axis=0, tiled=True)  21.1 us
    all_to_all x1, blocking collectives, body(): lax.all_to_all(parts, 'row', split_axis=2, concat_axis=2, tiled=True)  19.7 us
    all_to_all x1, starting transfers between devices, body(): lax.all_to_all(stacked_field, 'row', split_axis=1, concat_axis=3, tiled=T...  11.7 us
    another operation x16, other arithmetic  6.5 us
  transfers between devices with their start and end apart: 3, of which 3 were waited for; matrix products, arithmetic and copies ran while one was open for 1% of the time, Pallas kernels for 0%

profile of v7, /device:TPU:1, one launch (start us, length us, event | category | flops | bytes accessed | tf_op | source)
XLA Modules:
  0.0 307.8 jit_solution(9407051243248659025)
XLA Ops:
  8.5 1.1 multiply_convert_fusion
  10.7 1.1 copy.128
  11.8 22.2 %all-to-all-start = ((bf16[64,2,16,128]{3,2,1,0:T(8,128)(2,1)}), bf16[64,2,16,128]{3,2,1,0:T(8,128)(2,1)S(1)}, u32[]{:S(2)}, u32[]{:S(2)}) async-start(bf16[64,2,16,128]{3,2,1,0:T(8,128)(2,1)} %copy.128), calls=%async_computation | async-start | bytes 1048576 | tf_op jit(solution)/shard_map/all_to_all | solution.py:198
  34.8 21.1 %all-to-all-done = bf16[64,2,16,128]{3,2,1,0:T(8,128)(2,1)S(1)} async-done(((bf16[64,2,16,128]{3,2,1,0:T(8,128)(2,1)}), bf16[64,2,16,128]{3,2,1,0:T(8,128)(2,1)S(1)}, u32[]{:S(2)}, u32[]{:S(2)}) %all-to-all-start) | async-done | bytes 524320 | tf_op jit(solution)/shard_map/all_to_all | solution.py:198
  56.6 0.8 pad_maximum_fusion.7
  57.5 0.6 fusion.181
  59.4 0.6 gather_fusion
  61.6 105.1 %all-gather.2.cloned.1.call-done = bf16[2,64,128,128]{3,2,1,0:T(8,128)(2,1)} async-done(((bf16[2,8,128,128]{3,2,1,0:T(8,128)(2,1)}), bf16[2,64,128,128]{3,2,1,0:T(8,128)(2,1)}) %all-gather.2.cloned.1.call-update) | async-done | bytes 4194320 | tf_op jit(solution)/shard_map/all_gather | solution.py:218
  166.7 4.5 %convolution_multiply_fusion = f32[16,16384]{1,0:T(8,128)S(1)} fusion(bf16[16,128]{1,0:T(8,128)(2,1)S(1)} %reshape.891, bf16[16,8,128,128]{3,2,1,0:T(8,128)(2,1)} %bitcast.209, f32[]{:T(128)} %bitcast.39), kind=kOutput, calls=%fused_computation.1 | convolution fusion | flops 67371008 | bytes 5246980 | tf_op jit(solution)/shard_map/dot_general | solution.py:221
  171.4 1.6 fusion.20
  173.0 0.5 convolution_bitcast_fusion.5
  173.4 0.7 subtract_convert_fusion.5
  174.3 0.9 convolution_bitcast_fusion.4
  175.2 0.7 subtract_convert_fusion.4
  176.3 1.2 copy.255
  177.5 0.7 subtract_convert_fusion.3
  178.3 0.5 fusion.6
  178.8 1.7 copy.139
  180.4 11.7 %all-to-all-start.1 = ((bf16[2,64,32,128]{3,2,0,1:T(8,128)(2,1)}), bf16[2,64,32,128]{3,2,0,1:T(8,128)(2,1)S(1)}, u32[]{:S(2)}, u32[]{:S(2)}) async-start(bf16[2,64,32,128]{3,2,0,1:T(8,128)(2,1)} %copy.139), calls=%async_computation.1 | async-start | bytes 2097152 | tf_op jit(solution)/shard_map/all_to_all | solution.py:227
  193.1 53.6 %all-to-all-done.1 = bf16[2,64,32,128]{3,2,0,1:T(8,128)(2,1)S(1)} async-done(((bf16[2,64,32,128]{3,2,0,1:T(8,128)(2,1)}), bf16[2,64,32,128]{3,2,0,1:T(8,128)(2,1)S(1)}, u32[]{:S(2)}, u32[]{:S(2)}) %all-to-all-start.1) | async-done | bytes 1048608 | tf_op jit(solution)/shard_map/all_to_all | solution.py:227
  246.6 0.9 convolution_bitcast_fusion.2
  248.6 0.5 convolution_bitcast_fusion
  249.4 0.5 fusion.5
  250.4 1.1 fusion.180
  251.8 0.8 fusion.177
  252.6 1.8 fusion.43
  254.5 1.2 fusion.4
  256.6 19.7 %all_to_all.30 = f32[64,1,256]{2,1,0:T(1,128)S(1)} all-to-all(f32[64,1,256]{2,1,0:T(1,128)S(1)} %reshape.1069), channel_id=1, replica_groups=mesh['dir'=8,'row'=64] {'row'}, dimensions={0} | all-to-all | bytes 131072 | tf_op jit(solution)/shard_map/all_to_all | solution.py:265
  276.3 0.5 broadcast.1679
  276.8 0.8 reduce
  277.9 22.5 %all_to_all.31 = f32[2,8,1,16]{3,0,2,1:T(2,128)S(1)} all-to-all(f32[2,8,1,16]{3,0,2,1:T(2,128)S(1)} %copy.149), channel_id=1, replica_groups=mesh['dir'=8,'row'=64] {'dir'}, dimensions={1} | all-to-all | bytes 2048 | tf_op jit(solution)/shard_map/all_to_all | solution.py:267
  300.4 0.5 multiply_bitcast_fusion
  (71 shorter events, 8.8 us)
Async XLA Ops:
  11.8 44.1 %all-to-all-start = ((bf16[64,2,16,128]{3,2,1,0:T(8,128)(2,1)}), bf16[64,2,16,128]{3,2,1,0:T(8,128)(2,1)S(1)}, u32[]{:S(2)}, u32[]{:S(2)}) async-start(bf16[64,2,16,128]{3,2,1,0:T(8,128)(2,1)} %copy.128), calls=%async_computation | async-start | bytes 1048576 | tf_op jit(solution)/shard_map/all_to_all | solution.py:198
  34.0 132.6 %all-gather.2.cloned.1.call-start = ((), (), s32[]{:S(2)}) async-start(), calls=%async_computation.4 | async-start | bytes 4718592 | tf_op jit(solution)/shard_map/all_gather | solution.py:218
  55.9 1.5 copy-start.3
  178.7 14.2 %copy-start.1 = (s32[1,8192]{1,0:T(1,128)S(1)}, s32[1,8192]{1,0:T(1,128)}, u32[]{:S(2)}) copy-start(s32[1,8192]{1,0:T(1,128)} %param.9) | copy-start | bytes 98308
  180.4 66.2 %all-to-all-start.1 = ((bf16[2,64,32,128]{3,2,0,1:T(8,128)(2,1)}), bf16[2,64,32,128]{3,2,0,1:T(8,128)(2,1)S(1)}, u32[]{:S(2)}, u32[]{:S(2)}) async-start(bf16[2,64,32,128]{3,2,0,1:T(8,128)(2,1)} %copy.139), calls=%async_computation.1 | async-start | bytes 2097152 | tf_op jit(solution)/shard_map/all_to_all | solution.py:227
  254.4 1.2 copy-start
  254.4 1.2 copy-start.2
Sparse Core Ops, SparseCore 0:
  57.6 109.0 all-gather.1
